TPU v7x, 1024 devices: a whole 8x8x8 slice. The times are simulated.
1024 devices in a mesh: ctx: 64 (over y, z), tp: 16 (over x, core).
Axes of the slice: x: 8, y: 8, z: 8, core: 2. Of those that a mesh axis runs over, the one named last changes fastest.
Arguments:
- x_in: bfloat16 [4096, 8192], P('ctx', 'tp'), may hold values from -6 to 6
- z_in: bfloat16 [4096, 8192], P('ctx', 'tp'), may hold values from -6 to 6
- b_in: bfloat16 [4096, 4, 256], P('ctx'), may hold values from -6 to 6
- c_in: bfloat16 [4096, 4, 256], P('ctx'), may hold values from -6 to 6
- conv_x: bfloat16 [4, 8192], P(None, 'tp'), may hold values from -3 to 3
- conv_bc: bfloat16 [4, 2, 4, 256], replicated, may hold values from -3 to 3
- dt_raw: float32 [4096, 128], P('ctx', 'tp'), may hold values from -5 to 5
- dt_bias: float32 [128], P('tp'), may hold values from -1 to 1
- decay_rate: float32 [128], P('tp'), may hold values from 1.2207031e-05 to 0.05
- d_skip: float32 [128], P('tp'), may hold values from 0.5 to 1.5
- norm_gain: float32 [8192], P('tp'), may hold values from 0.1 to 1.9
- w_out: bfloat16 [8192, 8192], P('tp'), may hold values from -0.0625 to 0.0625
Outputs:
- mixed: bfloat16 [4096, 8192], P('ctx', 'tp')
All inputs are finite; a program needn't handle non-finite values.
Results may differ from a plain program's by a relative error of at most 0.022.
Values may be sent and summed in bfloat16 or wider, within the bound.
No kernel may reach another device: no remote copies, remote signals or barrier semaphores. Data moves between devices by JAX's collectives and lax.ppermute only.
A program may use at most 128 MiB of HBM per device.

v0:
```python
import jax
import jax.numpy as jnp
from jax import lax
from jax.sharding import PartitionSpec as P

HEADS = 128
HEAD_DIM = 64
STATE = 256
GROUPS = 4
CONV = 4


def shifted(block, axis, distance):
    devices = range(lax.axis_size(axis))
    route = [(i - distance, i) for i in devices if i - distance in devices]
    return lax.ppermute(block, axis, route)


def carried_in(value, axis, join, neutral):
    count, mine = (lax.axis_size(axis), lax.axis_index(axis))
    pieces = jax.tree.map(lambda part: lax.all_gather(part, axis), value)
    total = jax.tree.map(
        lambda part, zero: jnp.full_like(part, 0) + jnp.asarray(zero, part.dtype), value, neutral
    )

    def turn(position, total):
        longer = join(total, jax.tree.map(lambda part: part[position], pieces))
        return jax.tree.map(lambda new, old: jnp.where(position < mine, new, old), longer, total)

    return lax.fori_loop(0, count - 1, turn, total)


def causal_conv(tail, sequence, taps):
    length = sequence.shape[0]
    padded = jnp.concatenate([tail, sequence], 0).astype(jnp.float32)
    kernel = taps.astype(jnp.float32)
    total = jnp.zeros(sequence.shape, jnp.float32)
    for offset in range(taps.shape[0]):
        total = total + padded[offset : offset + length] * kernel[offset]
    return jax.nn.silu(total).astype(jnp.bfloat16)


def chain(earlier, later):
    return (earlier[0] * later[0], later[0][:, None, None] * earlier[1] + later[1])


def local(
    x_in, z_in, b_in, c_in, conv_x, conv_bc, dt_raw, dt_bias, decay_rate, d_skip, norm_gain, w_out
):
    length, channels = x_in.shape
    heads_here = dt_raw.shape[1]
    per_group = HEADS // GROUPS
    local_groups = max(heads_here // per_group, 1)
    repeat = heads_here // local_groups
    first_group = lax.axis_index("tp") * heads_here // per_group
    b_here = lax.dynamic_slice_in_dim(b_in, first_group, local_groups, 1).reshape(
        length, local_groups * STATE
    )
    c_here = lax.dynamic_slice_in_dim(c_in, first_group, local_groups, 1).reshape(
        length, local_groups * STATE
    )
    taps_here = lax.dynamic_slice_in_dim(conv_bc, first_group, local_groups, 2).reshape(
        CONV, 2 * local_groups * STATE
    )
    joined = jnp.concatenate([b_here, c_here], 1)
    x_tail, joined_tail = shifted(
        (x_in[length - CONV + 1 :], joined[length - CONV + 1 :]), "ctx", 1
    )
    xconv = causal_conv(x_tail, x_in, conv_x).reshape(length, heads_here, HEAD_DIM)
    joined_conv = causal_conv(joined_tail, joined, taps_here)
    bconv = joined_conv[:, : local_groups * STATE].reshape(length, local_groups, STATE)
    cconv = joined_conv[:, local_groups * STATE :].reshape(length, local_groups, STATE)
    delta = jax.nn.softplus(dt_raw + dt_bias[None, :])
    rate = -decay_rate[None, :] * delta
    cumulative = jnp.cumsum(rate, axis=0)
    along = cumulative.T
    causal = (jnp.arange(length)[:, None] >= jnp.arange(length)[None, :])[None]
    spread = along[:, :, None] - along[:, None, :]
    factor = jnp.where(causal, jnp.exp(jnp.where(causal, spread, 0.0)), 0.0) * delta.T[:, None, :]
    intersection = jnp.einsum("tgn,sgn->gts", cconv, bconv, preferred_element_type=jnp.float32)
    intersection = jnp.repeat(intersection, repeat, axis=0)
    mixing = (intersection * factor).astype(jnp.bfloat16)
    inner_out = jnp.einsum("hts,shp->thp", mixing, xconv, preferred_element_type=jnp.float32)
    tail_weight = jnp.exp(cumulative[-1][None, :] - cumulative) * delta
    weighted = (tail_weight[:, :, None] * xconv.astype(jnp.float32)).astype(jnp.bfloat16)
    keys_head = jnp.repeat(bconv, repeat, axis=1)
    local_state = jnp.einsum(
        "shp,shn->hpn", weighted, keys_head, preferred_element_type=jnp.float32
    )
    block_decay = jnp.exp(cumulative[-1])
    identity = (jnp.ones((heads_here,), jnp.float32), jnp.zeros(local_state.shape, jnp.float32))
    scanned = carried_in((block_decay, local_state), "ctx", chain, identity)
    incoming = scanned[1]
    queries = jnp.repeat(cconv, repeat, axis=1).astype(jnp.float32)
    carried = (
        jnp.einsum("thn,hpn->thp", queries, incoming, precision=lax.Precision.HIGHEST)
        * jnp.exp(cumulative)[:, :, None]
    )
    ssm_out = inner_out + carried + d_skip[None, :, None] * xconv.astype(jnp.float32)
    gated = ssm_out.reshape(length, channels) * jax.nn.silu(z_in.astype(jnp.float32))
    norm_size = per_group * HEAD_DIM
    grouped = gated.reshape(length, local_groups, channels // local_groups)
    partial_squares = jnp.sum(grouped * grouped, axis=-1)
    board = jnp.zeros((length, GROUPS), jnp.float32)
    board = lax.dynamic_update_slice_in_dim(board, partial_squares, first_group, 1)
    board = lax.psum(board, "tp")
    squares = lax.dynamic_slice_in_dim(board, first_group, local_groups, 1)
    scale = lax.rsqrt(squares / norm_size + 1e-05)
    hidden = ((grouped * scale[:, :, None]).reshape(length, channels) * norm_gain[None, :]).astype(
        jnp.bfloat16
    )
    partial_out = jnp.dot(hidden, w_out, preferred_element_type=jnp.float32)
    summed = lax.psum_scatter(
        partial_out.astype(jnp.bfloat16), "tp", scatter_dimension=1, tiled=True
    )
    return summed


def solution(mesh):
    return jax.shard_map(
        local,
        mesh=mesh,
        in_specs=(
            P("ctx", "tp"),
            P("ctx", "tp"),
            P("ctx", None, None),
            P("ctx", None, None),
            P(None, "tp"),
            P(),
            P("ctx", "tp"),
            P("tp"),
            P("tp"),
            P("tp"),
            P("tp"),
            P("tp", None),
        ),
        out_specs=P("ctx", "tp"),
        check_vma=False,
    )
```

profile of v0, /device:TPU:1, one launch (start us, length us, event | category | flops | bytes accessed | tf_op | source)
XLA Modules:
  0.0 437.1 jit_solution(15187177319373401824)
XLA Ops:
  7.3 5.7 %collective-permute-start = (bf16[3,512]{1,0:T(4,128)(2,1)S(1)}, bf16[3,512]{1,0:T(4,128)(2,1)S(1)}, u32[]{:S(2)}, u32[]{:S(2)}) collective-permute-start(bf16[3,512]{1,0:T(4,128)(2,1)S(1)} %slice.68), channel_id=1, source_target_pairs={{0,16},{16,32},{32,48},{48,64},{64,80},{80,96},{96,112},{112,128},... | collective-permute-start | bytes 9224 | tf_op jit(solution)/shard_map/ppermute | solution.py:16
  14.2 4.9 %collective-permute-start.1 = (bf16[3,512]{1,0:T(4,128)(2,1)S(1)}, bf16[3,512]{1,0:T(4,128)(2,1)S(1)}, u32[]{:S(2)}, u32[]{:S(2)}) collective-permute-start(bf16[3,512]{1,0:T(4,128)(2,1)S(1)} %pad_maximum_fusion), channel_id=1, source_target_pairs={{0,16},{16,32},{32,48},{48,64},{64,80},{80,96},{96,112},{112,128},... | collective-permute-start | bytes 9224 | tf_op jit(solution)/shard_map/ppermute | solution.py:16
  25.7 43.8 %all-gather.1 = f32[64,1,8]{2,1,0:T(1,128)S(1)} all-gather(f32[1,1,8]{2,1,0:T(1,128)S(1)} %get-tuple-element.131), channel_id=1, replica_groups=mesh['ctx'=64,'tp'=16] {'ctx'}, dimensions={0}, use_global_device_ids=true | all-gather | bytes 2080 | tf_op jit(solution)/shard_map/all_gather | solution.py:21
  69.6 192.5 %all-gather.4.cloned.1.call-done = f32[512,64,256]{2,1,0:T(8,128)} async-done(((f32[8,64,256]{2,1,0:T(8,128)}), f32[512,64,256]{2,1,0:T(8,128)}) %all-gather.4.cloned.1.call-update) | async-done | bytes 33554448 | tf_op jit(solution)/shard_map/all_gather | solution.py:21
  262.1 76.7 %while.14 = (s32[]{:T(128)}, f32[8,64,256]{2,1,0:T(8,128)S(1)}, s32[]{:T(128)}, f32[64,8]{1,0:T(8,128)S(1)}, f32[64,8,64,256]{3,2,1,0:T(8,128)}, /*index=5*/s32[]{:T(128)}, s32[]{:T(128)}) while((s32[]{:T(128)}, f32[8,64,256]{2,1,0:T(8,128)S(1)}, s32[]{:T(128)}, f32[64,8]{1,0:T(8,128)S(1)}, f32[64,8,64,256]{3,2,1,0:T(8,128)}, ...), condition=%wide.region_2.3_spmd.clone, body=%wide.region_1.2_spmd.clone.sunk | while | flops 524292 | bytes 1573073 | solution.py:30
  263.3 1.2 fusion.43
  267.0 1.2 fusion.43
  268.2 1.2 fusion.43
  271.8 1.2 fusion.43
  273.0 1.2 fusion.43
  276.7 1.2 fusion.43
  277.9 1.2 fusion.43
  281.6 1.2 fusion.43
  285.2 1.2 fusion.43
  286.4 1.2 fusion.43
  290.1 1.2 fusion.43
  291.3 1.2 fusion.43
  295.0 1.2 fusion.43
  296.2 1.2 fusion.43
  299.8 1.2 fusion.43
  301.1 1.2 fusion.43
  304.7 1.2 fusion.43
  308.4 1.2 fusion.43
  309.6 1.2 fusion.43
  313.2 1.2 fusion.43
  314.5 1.2 fusion.43
  318.1 1.2 fusion.43
  319.3 1.2 fusion.43
  323.0 1.2 fusion.43
  339.8 23.7 %psum.7 = f32[64,4]{0,1:T(4,128)S(1)} all-reduce(f32[64,4]{0,1:T(4,128)S(1)} %dynamic_update_slice.3), channel_id=1, replica_groups=mesh['ctx'=64,'tp'=16] {'tp'}, use_global_device_ids=true, to_apply=%region_4.5 | all-reduce | flops 256 | bytes 2048 | tf_op jit(solution)/shard_map/psum | solution.py:106
  363.5 6.0 %convolution_convert_fusion = bf16[64,8192]{1,0:T(8,128)(2,1)} fusion(bf16[512,8192]{1,0:T(8,128)(2,1)} %param.25, f32[512]{0:T(512)S(1)} %copy-done.1, f32[64]{0:T(128)S(1)} %rsqrt_bitcast_fusion, f32[64,512]{1,0:T(8,128)S(1)} %copy.49, bf16[64,512]{1,0:T(8,128)(2,1)S(1)} %copy-done), kind=kOutput, calls=%fused_computation.3 | convolution fusion | flops 537690112 | bytes 9636096 | tf_op jit(solution)/shard_map/dot_general | solution.py:112
  369.5 60.7 %reduce-scatter.2.cloned.1.call-done = bf16[64,512]{1,0:T(8,128)(2,1)} async-done(((bf16[64,8192]{1,0:T(8,128)(2,1)}), bf16[64,512]{1,0:T(8,128)(2,1)}) %reduce-scatter.2.cloned.1.call-update) | async-done | bytes 65552 | tf_op jit(solution)/shard_map/reduce_scatter | solution.py:113
  (149 shorter events, 55.9 us)
Async XLA Ops:
  6.5 332.6 %copy-start.2 = (f32[8]{0:T(128)S(1)}, f32[8]{0:T(128)}, u32[]{:S(2)}) copy-start(f32[8]{0:T(128)} %param.23) | copy-start | bytes 100
  6.5 333.0 %copy-start = (bf16[64,512]{1,0:T(8,128)(2,1)S(1)}, bf16[64,512]{1,0:T(8,128)(2,1)}, u32[]{:S(2)}) copy-start(bf16[64,512]{1,0:T(8,128)(2,1)} %param.15) | copy-start | bytes 196612
  6.5 357.0 %copy-start.1 = (f32[512]{0:T(512)S(1)}, f32[512]{0:T(512)}, u32[]{:S(2)}) copy-start(f32[512]{0:T(512)} %param.24) | copy-start | bytes 6148
  6.5 255.5 %all-gather.4.cloned.1.call-start = ((), (), s32[]{:S(2)}) async-start(), calls=%async_computation.2 | async-start | bytes 34078720 | tf_op jit(solution)/shard_map/all_gather | solution.py:21
  7.3 16.0 %collective-permute-start = (bf16[3,512]{1,0:T(4,128)(2,1)S(1)}, bf16[3,512]{1,0:T(4,128)(2,1)S(1)}, u32[]{:S(2)}, u32[]{:S(2)}) collective-permute-start(bf16[3,512]{1,0:T(4,128)(2,1)S(1)} %slice.68), channel_id=1, source_target_pairs={{0,16},{16,32},{32,48},{48,64},{64,80},{80,96},{96,112},{112,128},... | collective-permute-start | bytes 9224 | tf_op jit(solution)/shard_map/ppermute | solution.py:16
  14.2 9.0 %collective-permute-start.1 = (bf16[3,512]{1,0:T(4,128)(2,1)S(1)}, bf16[3,512]{1,0:T(4,128)(2,1)S(1)}, u32[]{:S(2)}, u32[]{:S(2)}) collective-permute-start(bf16[3,512]{1,0:T(4,128)(2,1)S(1)} %pad_maximum_fusion), channel_id=1, source_target_pairs={{0,16},{16,32},{32,48},{48,64},{64,80},{80,96},{96,112},{112,128},... | collective-permute-start | bytes 9224 | tf_op jit(solution)/shard_map/ppermute | solution.py:16
  25.5 404.8 %reduce-scatter.2.cloned.1.call-start = ((), (), s32[]{:S(2)}) async-start(), calls=%async_computation.1 | async-start | bytes 1114112 | tf_op jit(solution)/shard_map/reduce_scatter | solution.py:113
Sparse Core Ops, SparseCore 0:
  25.6 236.4 all-gather.3
  369.7 60.5 reduce-scatter.1
where the time goes:
time: 441 us; the launch traced here: 437 us
  waiting for transfers between devices  253 us (57%)
  other arithmetic  78.4 us (18%)
  blocking collectives  67.6 us (15%)
  between operations  13.6 us (3%)
  starting transfers between devices  10.7 us (2%)
  matrix products  7.77 us (2%)
    all_gather x1, waiting for transfers between devices, carried_in(): pieces = jax.tree.map(lambda part: lax.all_gather(part, axis), value)  192 us
    select_n x63, other arithmetic, turn(): jnp.where(position < mine, new, old)  74.1 us
    reduce_scatter x1, waiting for transfers between devices, local(): lax.psum_scatter(partial_out.astype(jnp.bfloat16), 'tp', scatter_dimensio...  60.7 us
    all_gather x1, blocking collectives, carried_in(): pieces = jax.tree.map(lambda part: lax.all_gather(part, axis), value)  43.8 us
    psum x1, blocking collectives, local(): board = lax.psum(board, 'tp')  23.7 us
    ppermute x2, starting transfers between devices, shifted(): return lax.ppermute(block, axis, route)  10.6 us
  transfers between devices with their start and end apart: 4, of which 2 were waited for; matrix products, arithmetic and copies ran while one was open for 1% of the time, Pallas kernels for 0%

commit v1 on v0

--- a/solution.py
+++ b/solution.py
@@ -8,6 +8,7 @@
 STATE = 256
 GROUPS = 4
 CONV = 4
+SIDE = 128
 
 
 def shifted(block, axis, distance):
@@ -16,18 +17,14 @@
     return lax.ppermute(block, axis, route)
 
 
-def carried_in(value, axis, join, neutral):
-    count, mine = (lax.axis_size(axis), lax.axis_index(axis))
-    pieces = jax.tree.map(lambda part: lax.all_gather(part, axis), value)
-    total = jax.tree.map(
-        lambda part, zero: jnp.full_like(part, 0) + jnp.asarray(zero, part.dtype), value, neutral
-    )
-
-    def turn(position, total):
-        longer = join(total, jax.tree.map(lambda part: part[position], pieces))
-        return jax.tree.map(lambda new, old: jnp.where(position < mine, new, old), longer, total)
-
-    return lax.fori_loop(0, count - 1, turn, total)
+def group_sum(value, axis, span):
+    total = value
+    step = 1
+    while step < span:
+        route = [(i, i ^ step) for i in range(lax.axis_size(axis))]
+        total = total + lax.ppermute(total, axis, route)
+        step *= 2
+    return total
 
 
 def causal_conv(tail, sequence, taps):
@@ -40,8 +37,12 @@
     return jax.nn.silu(total).astype(jnp.bfloat16)
 
 
-def chain(earlier, later):
-    return (earlier[0] * later[0], later[0][:, None, None] * earlier[1] + later[1])
+def split3(value):
+    hi = value.astype(jnp.bfloat16)
+    rest = value - hi.astype(jnp.float32)
+    mid = rest.astype(jnp.bfloat16)
+    lo = (rest - mid.astype(jnp.float32)).astype(jnp.bfloat16)
+    return hi, mid, lo
 
 
 def local(
@@ -83,28 +84,46 @@
     inner_out = jnp.einsum("hts,shp->thp", mixing, xconv, preferred_element_type=jnp.float32)
     tail_weight = jnp.exp(cumulative[-1][None, :] - cumulative) * delta
     weighted = (tail_weight[:, :, None] * xconv.astype(jnp.float32)).astype(jnp.bfloat16)
-    keys_head = jnp.repeat(bconv, repeat, axis=1)
-    local_state = jnp.einsum(
-        "shp,shn->hpn", weighted, keys_head, preferred_element_type=jnp.float32
+
+    cum_last = cumulative[-1]
+    side = jnp.zeros((length, SIDE), jnp.bfloat16)
+    side = side.at[0:3, 0:heads_here].set(jnp.stack(split3(cum_last)))
+    packet = jnp.concatenate(
+        [weighted.reshape(length, channels), bconv.reshape(length, local_groups * STATE), side], 1
     )
-    block_decay = jnp.exp(cumulative[-1])
-    identity = (jnp.ones((heads_here,), jnp.float32), jnp.zeros(local_state.shape, jnp.float32))
-    scanned = carried_in((block_decay, local_state), "ctx", chain, identity)
-    incoming = scanned[1]
-    queries = jnp.repeat(cconv, repeat, axis=1).astype(jnp.float32)
-    carried = (
-        jnp.einsum("thn,hpn->thp", queries, incoming, precision=lax.Precision.HIGHEST)
-        * jnp.exp(cumulative)[:, :, None]
+    gathered = lax.all_gather(packet, "ctx")
+    blocks = gathered.shape[0]
+    mine = lax.axis_index("ctx")
+    w_all = gathered[:, :, :channels]
+    b_all = gathered[:, :, channels : channels + local_groups * STATE]
+    pieces = gathered[:, 0:3, channels + local_groups * STATE :][:, :, :heads_here].astype(
+        jnp.float32
     )
+    lasts = pieces[:, 0] + pieces[:, 1] + pieces[:, 2]
+    order = jnp.arange(blocks)
+    between = (order[:, None] < order[None, :]) & (order[None, :] < mine)
+    span = jnp.sum(jnp.where(between[:, :, None], lasts[None, :, :], 0.0), axis=1)
+    gain = jnp.where((order < mine)[:, None], jnp.exp(span), 0.0)
+    gain = gain.reshape(blocks, 1, local_groups, repeat, 1)
+    w_scaled = (
+        w_all.reshape(blocks, length, local_groups, repeat, HEAD_DIM).astype(jnp.float32) * gain
+    )
+    b_all = b_all.reshape(blocks, length, local_groups, STATE)
+    scores = jnp.einsum("tgn,jsgn->gtjs", cconv, b_all, preferred_element_type=jnp.float32)
+    carried = jnp.einsum(
+        "gtjs,jsgrp->tgrp", scores, w_scaled, precision=lax.Precision.HIGHEST,
+        preferred_element_type=jnp.float32,
+    ).reshape(length, heads_here, HEAD_DIM)
+    carried = carried * jnp.exp(cumulative)[:, :, None]
     ssm_out = inner_out + carried + d_skip[None, :, None] * xconv.astype(jnp.float32)
     gated = ssm_out.reshape(length, channels) * jax.nn.silu(z_in.astype(jnp.float32))
     norm_size = per_group * HEAD_DIM
     grouped = gated.reshape(length, local_groups, channels // local_groups)
     partial_squares = jnp.sum(grouped * grouped, axis=-1)
-    board = jnp.zeros((length, GROUPS), jnp.float32)
-    board = lax.dynamic_update_slice_in_dim(board, partial_squares, first_group, 1)
-    board = lax.psum(board, "tp")
-    squares = lax.dynamic_slice_in_dim(board, first_group, local_groups, 1)
+    if local_groups == 1:
+        squares = group_sum(partial_squares, "tp", per_group // heads_here)
+    else:
+        squares = partial_squares
     scale = lax.rsqrt(squares / norm_size + 1e-05)
     hidden = ((grouped * scale[:, :, None]).reshape(length, channels) * norm_gain[None, :]).astype(
         jnp.bfloat16

time: 441 us -> 274 us (0.62)
  waiting for transfers between devices: 253 us -> 172 us
  blocking collectives: 67.6 us -> 0 us
  other arithmetic: 78.4 us -> 13 us
  matrix products: 7.77 us -> 40.2 us
  local copies, waits for them, and re-layouts: 3.88 us -> 16.9 us
  starting transfers between devices: 10.7 us -> 16.8 us
    all_gather x1, waiting for transfers between devices: 192 us -> 110 us  [local(): gathered = lax.all_gather(packet, 'ctx')]
    select_n x63 -> x1, other arithmetic: 74.1 us -> 0.01 us  [local(): gain = jnp.where((order < mine)[:, None], jnp.exp(span), 0.0)]
    all_gather x1 -> x0, blocking collectives: 43.8 us -> none  [carried_in(): pieces = jax.tree.map(lambda part: lax.all_gather(part, axis), value)]
    dot_general x2, matrix products: 1.38 us -> 33.8 us  [the longest x1 31.1 us: local(): jnp.einsum('gtjs,jsgrp->tgrp', scores, w_scaled, precision=lax.Precision....]
    psum x1 -> x0, blocking collectives: 23.7 us -> none  [local(): board = lax.psum(board, 'tp')]
    mul x63 -> x6, local copies, waits for them, and re-layouts: 0.59 us -> 13.5 us  [the longest x3 13.2 us: local(): w_all.reshape(blocks, length, local_groups, repeat, HEAD_DIM)]
    mul x0 -> x1, other arithmetic: none -> 6.84 us  [local(): w_all.reshape(blocks, length, local_groups, repeat, HEAD_DIM)]
    ppermute x0 -> x2, starting transfers between devices: none -> 6.13 us  [group_sum(): total = total + lax.ppermute(total, axis, route)]
  transfers between devices with their start and end apart: 4 -> 6, of which waited for: 2 -> 4; matrix products, arithmetic and copies ran while one was open for 1% -> 2% of each run, Pallas kernels for 0% -> 0%
where the time goes in v1:
time: 274 us; the launch traced here: 273 us
  waiting for transfers between devices  172 us (63%)
  matrix products  40.2 us (15%)
  local copies, waits for them, and re-layouts  16.9 us (6%)
  starting transfers between devices  16.8 us (6%)
  between operations  13.7 us (5%)
  other arithmetic  13 us (5%)
    all_gather x1, waiting for transfers between devices, local(): gathered = lax.all_gather(packet, 'ctx')  110 us
    reduce_scatter x1, waiting for transfers between devices, local(): lax.psum_scatter(partial_out.astype(jnp.bfloat16), 'tp', scatter_dimensio...  60.8 us
    dot_general x1, matrix products, local(): jnp.einsum('gtjs,jsgrp->tgrp', scores, w_scaled, precision=lax.Precision....  31.1 us
    mul x3, local copies, waits for them, and re-layouts, local(): w_all.reshape(blocks, length, local_groups, repeat, HEAD_DIM)  13.2 us
    ppermute x2, starting transfers between devices, shifted(): return lax.ppermute(block, axis, route)  10.6 us
    mul x1, other arithmetic, local(): w_all.reshape(blocks, length, local_groups, repeat, HEAD_DIM)  6.84 us
    ppermute x2, starting transfers between devices, group_sum(): total = total + lax.ppermute(total, axis, route)  6.13 us
    dot_general x1, matrix products, local(): partial_out = jnp.dot(hidden, w_out, preferred_element_type=jnp.float32)  5.98 us
  transfers between devices with their start and end apart: 6, of which 4 were waited for; matrix products, arithmetic and copies ran while one was open for 2% of the time, Pallas kernels for 0%

profile of v1, /device:TPU:1, one launch (start us, length us, event | category | flops | bytes accessed | tf_op | source)
XLA Modules:
  0.0 273.0 jit_solution(6359015139488210499)
XLA Ops:
  6.5 1.1 constant_dynamic-slice_fusion
  7.7 5.7 %collective-permute-start.1 = (bf16[3,512]{1,0:T(4,128)(2,1)S(1)}, bf16[3,512]{1,0:T(4,128)(2,1)S(1)}, u32[]{:S(2)}, u32[]{:S(2)}) collective-permute-start(bf16[3,512]{1,0:T(4,128)(2,1)S(1)} %pad_maximum_fusion.1), channel_id=1, source_target_pairs={{0,16},{16,32},{32,48},{48,64},{64,80},{80,96},{96,112},{112,128},... | collective-permute-start | bytes 9224 | tf_op jit(solution)/shard_map/ppermute | solution.py:17
  13.4 0.7 slice.108
  14.1 4.9 %collective-permute-start = (bf16[3,512]{1,0:T(4,128)(2,1)S(1)}, bf16[3,512]{1,0:T(4,128)(2,1)S(1)}, u32[]{:S(2)}, u32[]{:S(2)}) collective-permute-start(bf16[3,512]{1,0:T(4,128)(2,1)S(1)} %slice.108), channel_id=1, source_target_pairs={{0,16},{16,32},{32,48},{48,64},{64,80},{80,96},{96,112},{112,128},... | collective-permute-start | bytes 9224 | tf_op jit(solution)/shard_map/ppermute | solution.py:17
  19.0 0.7 neg.20
  19.7 0.8 broadcast_multiply_fusion
  20.7 0.7 dynamic-slice_convert_fusion
  21.5 0.8 fusion.55
  22.3 0.8 fusion.51
  23.2 0.1 mul.219
  23.3 0.1 mul.220
  23.6 0.9 maximum_convert_fusion
  24.6 0.6 pad_maximum_fusion
  25.5 0.1 copy.41
  25.6 0.1 fusion.42
  25.8 109.6 %all-gather.3.cloned.1.call-done = bf16[4096,896]{1,0:T(8,128)(2,1)} async-done(((bf16[64,896]{1,0:T(8,128)(2,1)}), bf16[4096,896]{1,0:T(8,128)(2,1)}) %all-gather.3.cloned.1.call-update) | async-done | bytes 7340048 | tf_op jit(solution)/shard_map/all_gather | solution.py:94
  135.3 2.7 fusion.2
  138.1 0.9 slice_convert_fusion
  139.1 0.2 select_reduce_fusion
  139.4 0.1 mul.222
  139.6 0.1 mul.223
  139.7 6.8 %convert_multiply_fusion = f32[64,64,512]{2,1,0:T(8,128)} fusion(bf16[64,64,896]{2,1,0:T(8,128)(2,1)} %bitcast.57, f32[64,512]{1,0:T(8,128)S(1)} %mul.223), kind=kLoop, calls=%fused_computation.3 | loop fusion | flops 4194304 | bytes 12713984 | tf_op jit(solution)/shard_map/mul | solution.py:109
  146.5 12.9 %mul.226 = f32[64,64,8,64]{3,2,1,0:T(8,128)} reshape(f32[64,64,512]{2,1,0:T(8,128)} %convert_multiply_fusion) | data formatting | bytes 16777216 | tf_op jit(solution)/shard_map/mul | solution.py:109
  159.4 31.1 %fusion.12 = f32[64,8,64]{0,2,1:T(8,128)S(1)} fusion(f32[64,64,64]{2,0,1:T(8,128)S(1)} %fusion.2, f32[64,64,8,64]{3,2,1,0:T(8,128)} %mul.226, f32[64,8]{0,1:T(8,128)S(1)} %copy.53), kind=kOutput, calls=%fused_computation.11 | convolution fusion | flops 1610645504 | bytes 9570304 | tf_op jit(solution)/shard_map/gtjs,jsgrp->tgrp/dot_general | solution.py:113
  190.6 0.3 fusion.6
  191.0 0.2 multiply_reduce_fusion
  191.2 3.0 %collective-permute-start.2 = (f32[64,1]{0,1:T(1,128)S(1)}, f32[64,1]{0,1:T(1,128)S(1)}, u32[]{:S(2)}, u32[]{:S(2)}) collective-permute-start(f32[64,1]{0,1:T(1,128)S(1)} %bitcast.74), channel_id=1, source_target_pairs={{0,1},{1,0},{2,3},{3,2},{4,5},{5,4},{6,7},{7,6},{8,9},{9,8},{10,11... | collective-permute-start | bytes 776 | tf_op jit(solution)/shard_map/ppermute | solution.py:25
  194.2 0.8 collective-permute-done.2
  195.0 3.1 %collective-permute-start.3 = (f32[64,1]{0,1:T(1,128)S(1)}, f32[64,1]{0,1:T(1,128)S(1)}, u32[]{:S(2)}, u32[]{:S(2)}) collective-permute-start(f32[64,1]{0,1:T(1,128)S(1)} %bitcast_add_fusion), channel_id=1, source_target_pairs={{0,2},{1,3},{2,0},{3,1},{4,6},{5,7},{6,4},{7,5},{8,10},{9,11},{10,... | collective-permute-start | bytes 776 | tf_op jit(solution)/shard_map/ppermute | solution.py:25
  198.1 1.2 collective-permute-done.3
  199.3 6.0 %convolution_convert_fusion = bf16[64,8192]{1,0:T(8,128)(2,1)} fusion(bf16[512,8192]{1,0:T(8,128)(2,1)} %param.25, f32[512]{0:T(512)S(1)} %copy-done.1, f32[64]{0:T(128)S(1)} %rsqrt_bitcast_fusion, f32[64,512]{1,0:T(8,128)S(1)} %copy.54, bf16[64,512]{1,0:T(8,128)(2,1)S(1)} %copy-done), kind=kOutput, calls=%fused_computation.2 | convolution fusion | flops 537690112 | bytes 9636096 | tf_op jit(solution)/shard_map/dot_general | solution.py:131
  205.3 60.8 %reduce-scatter.2.cloned.1.call-done = bf16[64,512]{1,0:T(8,128)(2,1)} async-done(((bf16[64,8192]{1,0:T(8,128)(2,1)}), bf16[64,512]{1,0:T(8,128)(2,1)}) %reduce-scatter.2.cloned.1.call-update) | async-done | bytes 65552 | tf_op jit(solution)/shard_map/reduce_scatter | solution.py:132
  (41 shorter events, 1.3 us)
Async XLA Ops:
  6.5 128.8 %all-gather.3.cloned.1.call-start = ((), (), s32[]{:S(2)}) async-start(), calls=%async_computation.2 | async-start | bytes 7454720 | tf_op jit(solution)/shard_map/all_gather | solution.py:94
  7.7 15.8 %collective-permute-start.1 = (bf16[3,512]{1,0:T(4,128)(2,1)S(1)}, bf16[3,512]{1,0:T(4,128)(2,1)S(1)}, u32[]{:S(2)}, u32[]{:S(2)}) collective-permute-start(bf16[3,512]{1,0:T(4,128)(2,1)S(1)} %pad_maximum_fusion.1), channel_id=1, source_target_pairs={{0,16},{16,32},{32,48},{48,64},{64,80},{80,96},{96,112},{112,128},... | collective-permute-start | bytes 9224 | tf_op jit(solution)/shard_map/ppermute | solution.py:17
  14.1 9.5 %collective-permute-start = (bf16[3,512]{1,0:T(4,128)(2,1)S(1)}, bf16[3,512]{1,0:T(4,128)(2,1)S(1)}, u32[]{:S(2)}, u32[]{:S(2)}) collective-permute-start(bf16[3,512]{1,0:T(4,128)(2,1)S(1)} %slice.108), channel_id=1, source_target_pairs={{0,16},{16,32},{32,48},{48,64},{64,80},{80,96},{96,112},{112,128},... | collective-permute-start | bytes 9224 | tf_op jit(solution)/shard_map/ppermute | solution.py:17
  25.3 240.9 %reduce-scatter.2.cloned.1.call-start = ((), (), s32[]{:S(2)}) async-start(), calls=%async_computation.1 | async-start | bytes 1114112 | tf_op jit(solution)/shard_map/reduce_scatter | solution.py:132
  159.4 31.2 %copy-start.2 = (f32[8]{0:T(128)S(1)}, f32[8]{0:T(128)}, u32[]{:S(2)}) copy-start(f32[8]{0:T(128)} %param.23) | copy-start | bytes 100
  159.4 31.6 %copy-start = (bf16[64,512]{1,0:T(8,128)(2,1)S(1)}, bf16[64,512]{1,0:T(8,128)(2,1)}, u32[]{:S(2)}) copy-start(bf16[64,512]{1,0:T(8,128)(2,1)} %param.15) | copy-start | bytes 196612
  159.4 39.9 %copy-start.1 = (f32[512]{0:T(512)S(1)}, f32[512]{0:T(512)}, u32[]{:S(2)}) copy-start(f32[512]{0:T(512)} %param.24) | copy-start | bytes 6148
  191.2 3.8 %collective-permute-start.2 = (f32[64,1]{0,1:T(1,128)S(1)}, f32[64,1]{0,1:T(1,128)S(1)}, u32[]{:S(2)}, u32[]{:S(2)}) collective-permute-start(f32[64,1]{0,1:T(1,128)S(1)} %bitcast.74), channel_id=1, source_target_pairs={{0,1},{1,0},{2,3},{3,2},{4,5},{5,4},{6,7},{7,6},{8,9},{9,8},{10,11... | collective-permute-start | bytes 776 | tf_op jit(solution)/shard_map/ppermute | solution.py:25
  195.0 4.3 %collective-permute-start.3 = (f32[64,1]{0,1:T(1,128)S(1)}, f32[64,1]{0,1:T(1,128)S(1)}, u32[]{:S(2)}, u32[]{:S(2)}) collective-permute-start(f32[64,1]{0,1:T(1,128)S(1)} %bitcast_add_fusion), channel_id=1, source_target_pairs={{0,2},{1,3},{2,0},{3,1},{4,6},{5,7},{6,4},{7,5},{8,10},{9,11},{10,... | collective-permute-start | bytes 776 | tf_op jit(solution)/shard_map/ppermute | solution.py:25
Sparse Core Ops, SparseCore 0:
  25.4 109.9 all-gather.2
  205.4 60.6 reduce-scatter.1

commit v2 on v1

--- a/solution.py
+++ b/solution.py
@@ -104,15 +104,21 @@
     between = (order[:, None] < order[None, :]) & (order[None, :] < mine)
     span = jnp.sum(jnp.where(between[:, :, None], lasts[None, :, :], 0.0), axis=1)
     gain = jnp.where((order < mine)[:, None], jnp.exp(span), 0.0)
-    gain = gain.reshape(blocks, 1, local_groups, repeat, 1)
-    w_scaled = (
-        w_all.reshape(blocks, length, local_groups, repeat, HEAD_DIM).astype(jnp.float32) * gain
+    gain = jnp.repeat(gain, HEAD_DIM, axis=1)[:, None, :]
+    w_scaled = (w_all.astype(jnp.float32) * gain).reshape(blocks * length, channels)
+    w_hi = w_scaled.astype(jnp.bfloat16)
+    w_lo = (w_scaled - w_hi.astype(jnp.float32)).astype(jnp.bfloat16)
+    b_flat = b_all.reshape(blocks * length, local_groups * STATE)
+    c_flat = cconv.reshape(length, local_groups * STATE)
+    scores = lax.dot_general(
+        c_flat, b_flat, (((1,), (1,)), ((), ())), preferred_element_type=jnp.float32
     )
-    b_all = b_all.reshape(blocks, length, local_groups, STATE)
-    scores = jnp.einsum("tgn,jsgn->gtjs", cconv, b_all, preferred_element_type=jnp.float32)
-    carried = jnp.einsum(
-        "gtjs,jsgrp->tgrp", scores, w_scaled, precision=lax.Precision.HIGHEST,
-        preferred_element_type=jnp.float32,
+    s_hi = scores.astype(jnp.bfloat16)
+    s_lo = (scores - s_hi.astype(jnp.float32)).astype(jnp.bfloat16)
+    carried = (
+        jnp.dot(s_hi, w_hi, preferred_element_type=jnp.float32)
+        + jnp.dot(s_lo, w_hi, preferred_element_type=jnp.float32)
+        + jnp.dot(s_hi, w_lo, preferred_element_type=jnp.float32)
     ).reshape(length, heads_here, HEAD_DIM)
     carried = carried * jnp.exp(cumulative)[:, :, None]
     ssm_out = inner_out + carried + d_skip[None, :, None] * xconv.astype(jnp.float32)

time: 274 us -> 234 us (0.85)
  matrix products: 40.2 us -> 9.65 us
  local copies, waits for them, and re-layouts: 16.9 us -> 6.31 us
    dot_general x2 -> x4, matrix products: 33.8 us -> 3.27 us  [the longest x1 0.86 us: local(): jnp.dot(s_hi, w_lo, preferred_element_type=jnp.float32)]
    mul x3 -> x1, local copies, waits for them, and re-layouts: 13.2 us -> 0.12 us  [local(): w_all.astype(jnp.float32) * gain]
    convert_element_type x0 -> x2, other arithmetic: none -> 4.34 us  [the longest x1 4.33 us: local(): w_lo = (w_scaled - w_hi.astype(jnp.float32)).astype(jnp.bfloat16)]
    mul x1, other arithmetic: 6.84 us -> 3.6 us  [local(): w_all.astype(jnp.float32) * gain]
  transfers between devices with their start and end apart: 6 -> 6, of which waited for: 4 -> 4; matrix products, arithmetic and copies ran while one was open for 2% -> 3% of each run, Pallas kernels for 0% -> 0%
where the time goes in v2:
time: 234 us; the launch traced here: 233 us
  waiting for transfers between devices  172 us (74%)
  starting transfers between devices  16.8 us (7%)
  other arithmetic  14.1 us (6%)
  between operations  13.7 us (6%)
  matrix products  9.65 us (4%)
  local copies, waits for them, and re-layouts  6.31 us (3%)
    all_gather x1, waiting for transfers between devices, local(): gathered = lax.all_gather(packet, 'ctx')  110 us
    reduce_scatter x1, waiting for transfers between devices, local(): lax.psum_scatter(partial_out.astype(jnp.bfloat16), 'tp', scatter_dimensio...  60.8 us
    ppermute x2, starting transfers between devices, shifted(): return lax.ppermute(block, axis, route)  10.6 us
    ppermute x2, starting transfers between devices, group_sum(): total = total + lax.ppermute(total, axis, route)  6.13 us
    dot_general x1, matrix products, local(): partial_out = jnp.dot(hidden, w_out, preferred_element_type=jnp.float32)  5.97 us
  transfers between devices with their start and end apart: 6, of which 4 were waited for; matrix products, arithmetic and copies ran while one was open for 3% of the time, Pallas kernels for 0%

profile of v2, /device:TPU:1, one launch (start us, length us, event | category | flops | bytes accessed | tf_op | source)
XLA Modules:
  0.0 233.0 jit_solution(3323069920077851223)
XLA Ops:
  6.5 0.7 slice.108
  7.2 5.7 %collective-permute-start = (bf16[3,512]{1,0:T(4,128)(2,1)S(1)}, bf16[3,512]{1,0:T(4,128)(2,1)S(1)}, u32[]{:S(2)}, u32[]{:S(2)}) collective-permute-start(bf16[3,512]{1,0:T(4,128)(2,1)S(1)} %slice.108), channel_id=1, source_target_pairs={{0,16},{16,32},{32,48},{48,64},{64,80},{80,96},{96,112},{112,128},... | collective-permute-start | bytes 9224 | tf_op jit(solution)/shard_map/ppermute | solution.py:17
  13.0 1.1 constant_dynamic-slice_fusion
  14.1 4.9 %collective-permute-start.1 = (bf16[3,512]{1,0:T(4,128)(2,1)S(1)}, bf16[3,512]{1,0:T(4,128)(2,1)S(1)}, u32[]{:S(2)}, u32[]{:S(2)}) collective-permute-start(bf16[3,512]{1,0:T(4,128)(2,1)S(1)} %pad_maximum_fusion.1), channel_id=1, source_target_pairs={{0,16},{16,32},{32,48},{48,64},{64,80},{80,96},{96,112},{112,128},... | collective-permute-start | bytes 9224 | tf_op jit(solution)/shard_map/ppermute | solution.py:17
  19.1 0.7 neg.20
  19.7 0.8 broadcast_multiply_fusion
  20.8 0.7 dynamic-slice_convert_fusion
  21.5 0.8 fusion.45
  22.4 0.8 fusion.41
  23.6 0.9 maximum_convert_fusion
  24.6 0.6 pad_maximum_fusion
  25.7 0.1 fusion.28
  25.8 109.6 %all-gather.3.cloned.1.call-done = bf16[4096,896]{1,0:T(8,128)(2,1)} async-done(((bf16[64,896]{1,0:T(8,128)(2,1)}), bf16[4096,896]{1,0:T(8,128)(2,1)}) %all-gather.3.cloned.1.call-update) | async-done | bytes 7340048 | tf_op jit(solution)/shard_map/all_gather | solution.py:94
  135.4 0.9 slice_convert_fusion
  136.3 1.7 slice.154
  138.1 0.2 select_reduce_fusion
  138.5 0.1 broadcast_in_dim.78
  138.7 0.7 fusion.26
  139.5 3.6 %convert_multiply_fusion = f32[64,64,512]{2,1,0:T(8,128)S(1)} fusion(bf16[64,64,896]{2,1,0:T(8,128)(2,1)} %bitcast.50, f32[64,512]{1,0:T(8,128)S(1)} %mul.214), kind=kLoop, calls=%fused_computation.4 | loop fusion | flops 4194304 | bytes 12713984 | tf_op jit(solution)/shard_map/mul | solution.py:108
  143.1 4.3 %fusion = (bf16[4096,512]{1,0:T(8,128)(2,1)}, bf16[4096,512]{1,0:T(8,128)(2,1)S(1)}) fusion(f32[64,64,512]{2,1,0:T(8,128)S(1)} %convert_multiply_fusion), kind=kLoop, calls=%fused_computation.3 | loop fusion | flops 8388608 | bytes 16777216 | tf_op jit(solution)/shard_map/convert_element_type | solution.py:110
  147.4 0.8 fusion.37
  148.2 0.8 convolution_add_fusion.1
  149.1 0.5 copy-done
  149.6 0.9 convolution_add_fusion
  150.6 0.3 fusion.2
  151.0 0.2 multiply_reduce_fusion
  151.2 3.0 %collective-permute-start.2 = (f32[64,1]{0,1:T(1,128)S(1)}, f32[64,1]{0,1:T(1,128)S(1)}, u32[]{:S(2)}, u32[]{:S(2)}) collective-permute-start(f32[64,1]{0,1:T(1,128)S(1)} %bitcast.68), channel_id=1, source_target_pairs={{0,1},{1,0},{2,3},{3,2},{4,5},{5,4},{6,7},{7,6},{8,9},{9,8},{10,11... | collective-permute-start | bytes 776 | tf_op jit(solution)/shard_map/ppermute | solution.py:25
  154.2 0.8 collective-permute-done.2
  155.0 3.1 %collective-permute-start.3 = (f32[64,1]{0,1:T(1,128)S(1)}, f32[64,1]{0,1:T(1,128)S(1)}, u32[]{:S(2)}, u32[]{:S(2)}) collective-permute-start(f32[64,1]{0,1:T(1,128)S(1)} %bitcast_add_fusion), channel_id=1, source_target_pairs={{0,2},{1,3},{2,0},{3,1},{4,6},{5,7},{6,4},{7,5},{8,10},{9,11},{10,... | collective-permute-start | bytes 776 | tf_op jit(solution)/shard_map/ppermute | solution.py:25
  158.1 1.2 collective-permute-done.3
  159.3 6.0 %convolution_convert_fusion = bf16[64,8192]{1,0:T(8,128)(2,1)} fusion(bf16[512,8192]{1,0:T(8,128)(2,1)} %param.25, f32[512]{0:T(512)S(1)} %copy-done.2, f32[64]{0:T(128)S(1)} %rsqrt_bitcast_fusion, f32[64,512]{1,0:T(8,128)S(1)} %copy.55, bf16[64,512]{1,0:T(8,128)(2,1)S(1)} %copy-done.1), kind=kOutput, calls=%fused_computation | convolution fusion | flops 537690112 | bytes 9636096 | tf_op jit(solution)/shard_map/dot_general | solution.py:137
  165.3 60.8 %reduce-scatter.2.cloned.1.call-done = bf16[64,512]{1,0:T(8,128)(2,1)} async-done(((bf16[64,8192]{1,0:T(8,128)(2,1)}), bf16[64,512]{1,0:T(8,128)(2,1)}) %reduce-scatter.2.cloned.1.call-update) | async-done | bytes 65552 | tf_op jit(solution)/shard_map/reduce_scatter | solution.py:138
  (47 shorter events, 1.9 us)
Async XLA Ops:
  6.5 128.8 %all-gather.3.cloned.1.call-start = ((), (), s32[]{:S(2)}) async-start(), calls=%async_computation.2 | async-start | bytes 7454720 | tf_op jit(solution)/shard_map/all_gather | solution.py:94
  7.2 16.4 %collective-permute-start = (bf16[3,512]{1,0:T(4,128)(2,1)S(1)}, bf16[3,512]{1,0:T(4,128)(2,1)S(1)}, u32[]{:S(2)}, u32[]{:S(2)}) collective-permute-start(bf16[3,512]{1,0:T(4,128)(2,1)S(1)} %slice.108), channel_id=1, source_target_pairs={{0,16},{16,32},{32,48},{48,64},{64,80},{80,96},{96,112},{112,128},... | collective-permute-start | bytes 9224 | tf_op jit(solution)/shard_map/ppermute | solution.py:17
  14.1 9.3 %collective-permute-start.1 = (bf16[3,512]{1,0:T(4,128)(2,1)S(1)}, bf16[3,512]{1,0:T(4,128)(2,1)S(1)}, u32[]{:S(2)}, u32[]{:S(2)}) collective-permute-start(bf16[3,512]{1,0:T(4,128)(2,1)S(1)} %pad_maximum_fusion.1), channel_id=1, source_target_pairs={{0,16},{16,32},{32,48},{48,64},{64,80},{80,96},{96,112},{112,128},... | collective-permute-start | bytes 9224 | tf_op jit(solution)/shard_map/ppermute | solution.py:17
  25.3 200.8 %reduce-scatter.2.cloned.1.call-start = ((), (), s32[]{:S(2)}) async-start(), calls=%async_computation.1 | async-start | bytes 1114112 | tf_op jit(solution)/shard_map/reduce_scatter | solution.py:138
  147.4 2.2 copy-start
  149.1 1.5 copy-start.3
  149.1 1.9 copy-start.1
  149.1 10.2 %copy-start.2 = (f32[512]{0:T(512)S(1)}, f32[512]{0:T(512)}, u32[]{:S(2)}) copy-start(f32[512]{0:T(512)} %param.24) | copy-start | bytes 6148
  151.2 3.8 %collective-permute-start.2 = (f32[64,1]{0,1:T(1,128)S(1)}, f32[64,1]{0,1:T(1,128)S(1)}, u32[]{:S(2)}, u32[]{:S(2)}) collective-permute-start(f32[64,1]{0,1:T(1,128)S(1)} %bitcast.68), channel_id=1, source_target_pairs={{0,1},{1,0},{2,3},{3,2},{4,5},{5,4},{6,7},{7,6},{8,9},{9,8},{10,11... | collective-permute-start | bytes 776 | tf_op jit(solution)/shard_map/ppermute | solution.py:25
  155.0 4.3 %collective-permute-start.3 = (f32[64,1]{0,1:T(1,128)S(1)}, f32[64,1]{0,1:T(1,128)S(1)}, u32[]{:S(2)}, u32[]{:S(2)}) collective-permute-start(f32[64,1]{0,1:T(1,128)S(1)} %bitcast_add_fusion), channel_id=1, source_target_pairs={{0,2},{1,3},{2,0},{3,1},{4,6},{5,7},{6,4},{7,5},{8,10},{9,11},{10,... | collective-permute-start | bytes 776 | tf_op jit(solution)/shard_map/ppermute | solution.py:25
Sparse Core Ops, SparseCore 0:
  25.4 109.9 all-gather.2
  165.5 60.6 reduce-scatter.1

commit v3 on v2

--- a/solution.py
+++ b/solution.py
@@ -135,9 +135,10 @@
         jnp.bfloat16
     )
     partial_out = jnp.dot(hidden, w_out, preferred_element_type=jnp.float32)
-    summed = lax.psum_scatter(
-        partial_out.astype(jnp.bfloat16), "tp", scatter_dimension=1, tiled=True
-    )
+    owners = lax.axis_size("tp")
+    pieces_out = partial_out.astype(jnp.bfloat16).reshape(length, owners, -1).transpose(1, 0, 2)
+    received = lax.all_to_all(pieces_out, "tp", 0, 0, tiled=True)
+    summed = jnp.sum(received.astype(jnp.float32), axis=0).astype(jnp.bfloat16)
     return summed
 
 

time: 234 us -> 209 us (0.89)
  waiting for transfers between devices: 172 us -> 112 us
  blocking collectives: 0 us -> 36.4 us
    reduce_scatter x1 -> x0, waiting for transfers between devices: 60.8 us -> none  [local(): lax.psum_scatter(partial_out.astype(jnp.bfloat16), 'tp', scatter_dimensio...]
    all_to_all x0 -> x1, blocking collectives: none -> 36.4 us  [local(): received = lax.all_to_all(pieces_out, 'tp', 0, 0, tiled=True)]
  transfers between devices with their start and end apart: 6 -> 5, of which waited for: 4 -> 3; matrix products, arithmetic and copies ran while one was open for 3% -> 3% of each run, Pallas kernels for 0% -> 0%
where the time goes in v3:
time: 209 us; the launch traced here: 208 us
  waiting for transfers between devices  112 us (54%)
  blocking collectives  36.4 us (17%)
  starting transfers between devices  16.8 us (8%)
  other arithmetic  14.8 us (7%)
  between operations  13.7 us (7%)
  matrix products  8.68 us (4%)
  local copies, waits for them, and re-layouts  6.41 us (3%)
    all_gather x1, waiting for transfers between devices, local(): gathered = lax.all_gather(packet, 'ctx')  110 us
    all_to_all x1, blocking collectives, local(): received = lax.all_to_all(pieces_out, 'tp', 0, 0, tiled=True)  36.4 us
    ppermute x2, starting transfers between devices, shifted(): return lax.ppermute(block, axis, route)  10.6 us
    ppermute x2, starting transfers between devices, group_sum(): total = total + lax.ppermute(total, axis, route)  6.13 us
    dot_general x1, matrix products, local(): partial_out = jnp.dot(hidden, w_out, preferred_element_type=jnp.float32)  5.01 us
    convert_element_type x1, other arithmetic, local(): w_lo = (w_scaled - w_hi.astype(jnp.float32)).astype(jnp.bfloat16)  4.33 us
  transfers between devices with their start and end apart: 5, of which 3 were waited for; matrix products, arithmetic and copies ran while one was open for 3% of the time, Pallas kernels for 0%

profile of v3, /device:TPU:1, one launch (start us, length us, event | category | flops | bytes accessed | tf_op | source)
XLA Modules:
  0.0 208.5 jit_solution(12216985471990322286)
XLA Ops:
  6.5 0.7 slice.108
  7.2 5.7 %collective-permute-start = (bf16[3,512]{1,0:T(4,128)(2,1)S(1)}, bf16[3,512]{1,0:T(4,128)(2,1)S(1)}, u32[]{:S(2)}, u32[]{:S(2)}) collective-permute-start(bf16[3,512]{1,0:T(4,128)(2,1)S(1)} %slice.108), channel_id=1, source_target_pairs={{0,16},{16,32},{32,48},{48,64},{64,80},{80,96},{96,112},{112,128},... | collective-permute-start | bytes 9224 | tf_op jit(solution)/shard_map/ppermute | solution.py:17
  13.0 1.1 constant_dynamic-slice_fusion
  14.1 4.9 %collective-permute-start.1 = (bf16[3,512]{1,0:T(4,128)(2,1)S(1)}, bf16[3,512]{1,0:T(4,128)(2,1)S(1)}, u32[]{:S(2)}, u32[]{:S(2)}) collective-permute-start(bf16[3,512]{1,0:T(4,128)(2,1)S(1)} %pad_maximum_fusion.1), channel_id=1, source_target_pairs={{0,16},{16,32},{32,48},{48,64},{64,80},{80,96},{96,112},{112,128},... | collective-permute-start | bytes 9224 | tf_op jit(solution)/shard_map/ppermute | solution.py:17
  19.1 0.7 neg.20
  19.7 0.8 broadcast_multiply_fusion
  20.8 0.7 dynamic-slice_convert_fusion
  21.5 0.8 fusion.45
  22.4 0.8 fusion.41
  23.6 0.9 maximum_convert_fusion
  24.6 0.7 pad_maximum_fusion
  25.7 109.6 %all-gather.3.cloned.1.call-done = bf16[4096,896]{1,0:T(8,128)(2,1)} async-done(((bf16[64,896]{1,0:T(8,128)(2,1)}), bf16[4096,896]{1,0:T(8,128)(2,1)}) %all-gather.3.cloned.1.call-update) | async-done | bytes 7340048 | tf_op jit(solution)/shard_map/all_gather | solution.py:94
  135.4 0.9 slice_convert_fusion
  136.3 1.7 slice.154
  138.1 0.2 select_reduce_fusion
  138.5 0.1 broadcast_in_dim.78
  138.7 0.8 fusion.26
  139.5 3.6 %convert_multiply_fusion = f32[64,64,512]{2,1,0:T(8,128)S(1)} fusion(bf16[64,64,896]{2,1,0:T(8,128)(2,1)} %bitcast.57, f32[64,512]{1,0:T(8,128)S(1)} %mul.214), kind=kLoop, calls=%fused_computation.4 | loop fusion | flops 4194304 | bytes 12713984 | tf_op jit(solution)/shard_map/mul | solution.py:108
  143.1 4.3 %fusion = (bf16[4096,512]{1,0:T(8,128)(2,1)}, bf16[4096,512]{1,0:T(8,128)(2,1)S(1)}) fusion(f32[64,64,512]{2,1,0:T(8,128)S(1)} %convert_multiply_fusion), kind=kLoop, calls=%fused_computation.3 | loop fusion | flops 8388608 | bytes 16777216 | tf_op jit(solution)/shard_map/convert_element_type | solution.py:110
  147.4 0.8 fusion.37
  148.2 0.8 convolution_add_fusion.1
  149.1 0.5 copy-done
  149.6 0.9 convolution_add_fusion
  150.6 0.3 fusion.2
  151.0 0.2 multiply_reduce_fusion
  151.2 3.0 %collective-permute-start.2 = (f32[64,1]{0,1:T(1,128)S(1)}, f32[64,1]{0,1:T(1,128)S(1)}, u32[]{:S(2)}, u32[]{:S(2)}) collective-permute-start(f32[64,1]{0,1:T(1,128)S(1)} %bitcast.77), channel_id=1, source_target_pairs={{0,1},{1,0},{2,3},{3,2},{4,5},{5,4},{6,7},{7,6},{8,9},{9,8},{10,11... | collective-permute-start | bytes 776 | tf_op jit(solution)/shard_map/ppermute | solution.py:25
  154.2 0.8 collective-permute-done.2
  155.0 3.1 %collective-permute-start.3 = (f32[64,1]{0,1:T(1,128)S(1)}, f32[64,1]{0,1:T(1,128)S(1)}, u32[]{:S(2)}, u32[]{:S(2)}) collective-permute-start(f32[64,1]{0,1:T(1,128)S(1)} %bitcast_add_fusion), channel_id=1, source_target_pairs={{0,2},{1,3},{2,0},{3,1},{4,6},{5,7},{6,4},{7,5},{8,10},{9,11},{10,... | collective-permute-start | bytes 776 | tf_op jit(solution)/shard_map/ppermute | solution.py:25
  158.1 1.2 collective-permute-done.3
  159.3 5.0 %convolution_convert_fusion = bf16[64,8192]{1,0:T(8,128)(2,1)S(1)} fusion(bf16[512,8192]{1,0:T(8,128)(2,1)} %param.25, f32[512]{0:T(512)S(1)} %copy-done.2, f32[64]{0:T(128)S(1)} %rsqrt_bitcast_fusion, f32[64,512]{1,0:T(8,128)S(1)} %copy.67, bf16[64,512]{1,0:T(8,128)(2,1)S(1)} %copy-done.1), kind=kOutput, calls=%fused_computation | convolution fusion | flops 537690112 | bytes 9636096 | tf_op jit(solution)/shard_map/dot_general | solution.py:137
  164.5 36.4 %all_to_all.5 = bf16[16,64,512]{2,1,0:T(8,128)(2,1)S(1)} all-to-all(bf16[16,64,512]{2,1,0:T(8,128)(2,1)S(1)} %bitcast.59), channel_id=1, replica_groups=mesh['ctx'=64,'tp'=16] {'tp'}, dimensions={0} | all-to-all | bytes 2097152 | tf_op jit(solution)/shard_map/all_to_all | solution.py:140
  200.9 0.8 reduce_sum.35
  (47 shorter events, 2.0 us)
Async XLA Ops:
  6.5 128.8 %all-gather.3.cloned.1.call-start = ((), (), s32[]{:S(2)}) async-start(), calls=%async_computation.1 | async-start | bytes 7454720 | tf_op jit(solution)/shard_map/all_gather | solution.py:94
  7.2 16.4 %collective-permute-start = (bf16[3,512]{1,0:T(4,128)(2,1)S(1)}, bf16[3,512]{1,0:T(4,128)(2,1)S(1)}, u32[]{:S(2)}, u32[]{:S(2)}) collective-permute-start(bf16[3,512]{1,0:T(4,128)(2,1)S(1)} %slice.108), channel_id=1, source_target_pairs={{0,16},{16,32},{32,48},{48,64},{64,80},{80,96},{96,112},{112,128},... | collective-permute-start | bytes 9224 | tf_op jit(solution)/shard_map/ppermute | solution.py:17
  14.1 9.3 %collective-permute-start.1 = (bf16[3,512]{1,0:T(4,128)(2,1)S(1)}, bf16[3,512]{1,0:T(4,128)(2,1)S(1)}, u32[]{:S(2)}, u32[]{:S(2)}) collective-permute-start(bf16[3,512]{1,0:T(4,128)(2,1)S(1)} %pad_maximum_fusion.1), channel_id=1, source_target_pairs={{0,16},{16,32},{32,48},{48,64},{64,80},{80,96},{96,112},{112,128},... | collective-permute-start | bytes 9224 | tf_op jit(solution)/shard_map/ppermute | solution.py:17
  147.4 2.2 %copy-start = (bf16[4096,512]{1,0:T(8,128)(2,1)S(1)}, bf16[4096,512]{1,0:T(8,128)(2,1)}, u32[]{:S(2)}) copy-start(bf16[4096,512]{1,0:T(8,128)(2,1)} %get-tuple-element.17) | copy-start | bytes 12582916
  149.1 1.5 copy-start.3
  149.1 1.9 copy-start.1
  149.1 10.2 %copy-start.2 = (f32[512]{0:T(512)S(1)}, f32[512]{0:T(512)}, u32[]{:S(2)}) copy-start(f32[512]{0:T(512)} %param.24) | copy-start | bytes 6148
  151.2 3.8 %collective-permute-start.2 = (f32[64,1]{0,1:T(1,128)S(1)}, f32[64,1]{0,1:T(1,128)S(1)}, u32[]{:S(2)}, u32[]{:S(2)}) collective-permute-start(f32[64,1]{0,1:T(1,128)S(1)} %bitcast.77), channel_id=1, source_target_pairs={{0,1},{1,0},{2,3},{3,2},{4,5},{5,4},{6,7},{7,6},{8,9},{9,8},{10,11... | collective-permute-start | bytes 776 | tf_op jit(solution)/shard_map/ppermute | solution.py:25
  155.0 4.3 %collective-permute-start.3 = (f32[64,1]{0,1:T(1,128)S(1)}, f32[64,1]{0,1:T(1,128)S(1)}, u32[]{:S(2)}, u32[]{:S(2)}) collective-permute-start(f32[64,1]{0,1:T(1,128)S(1)} %bitcast_add_fusion), channel_id=1, source_target_pairs={{0,2},{1,3},{2,0},{3,1},{4,6},{5,7},{6,4},{7,5},{8,10},{9,11},{10,... | collective-permute-start | bytes 776 | tf_op jit(solution)/shard_map/ppermute | solution.py:25
Sparse Core Ops, SparseCore 0:
  25.4 109.9 all-gather.2

commit v4 on v3

--- a/solution.py
+++ b/solution.py
@@ -12,7 +12,7 @@
 
 
 def shifted(block, axis, distance):
-    devices = range(lax.axis_size(axis))
+    devices = range(lax.psum(1, axis))
     route = [(i - distance, i) for i in devices if i - distance in devices]
     return lax.ppermute(block, axis, route)
 
@@ -43,6 +43,11 @@
     mid = rest.astype(jnp.bfloat16)
     lo = (rest - mid.astype(jnp.float32)).astype(jnp.bfloat16)
     return hi, mid, lo
+
+
+def split2(value):
+    hi = value.astype(jnp.bfloat16)
+    return hi, (value - hi.astype(jnp.float32)).astype(jnp.bfloat16)
 
 
 def local(
@@ -65,7 +70,7 @@
     )
     joined = jnp.concatenate([b_here, c_here], 1)
     x_tail, joined_tail = shifted(
-        (x_in[length - CONV + 1 :], joined[length - CONV + 1 :]), "ctx", 1
+        (x_in[length - CONV + 1 :], joined[length - CONV + 1 :]), ("cy", "cz"), 1
     )
     xconv = causal_conv(x_tail, x_in, conv_x).reshape(length, heads_here, HEAD_DIM)
     joined_conv = causal_conv(joined_tail, joined, taps_here)
@@ -88,38 +93,63 @@
     cum_last = cumulative[-1]
     side = jnp.zeros((length, SIDE), jnp.bfloat16)
     side = side.at[0:3, 0:heads_here].set(jnp.stack(split3(cum_last)))
+    width = local_groups * STATE
     packet = jnp.concatenate(
-        [weighted.reshape(length, channels), bconv.reshape(length, local_groups * STATE), side], 1
-    )
-    gathered = lax.all_gather(packet, "ctx")
+        [weighted.reshape(length, channels), bconv.reshape(length, width), side], 1
+    )
+    gathered = lax.all_gather(packet, "cz")
     blocks = gathered.shape[0]
-    mine = lax.axis_index("ctx")
+    mine = lax.axis_index("cz")
     w_all = gathered[:, :, :channels]
-    b_all = gathered[:, :, channels : channels + local_groups * STATE]
-    pieces = gathered[:, 0:3, channels + local_groups * STATE :][:, :, :heads_here].astype(
-        jnp.float32
-    )
+    b_flat = gathered[:, :, channels : channels + width].reshape(blocks * length, width)
+    pieces = gathered[:, 0:3, channels + width :][:, :, :heads_here].astype(jnp.float32)
     lasts = pieces[:, 0] + pieces[:, 1] + pieces[:, 2]
     order = jnp.arange(blocks)
     between = (order[:, None] < order[None, :]) & (order[None, :] < mine)
     span = jnp.sum(jnp.where(between[:, :, None], lasts[None, :, :], 0.0), axis=1)
     gain = jnp.where((order < mine)[:, None], jnp.exp(span), 0.0)
-    gain = jnp.repeat(gain, HEAD_DIM, axis=1)[:, None, :]
-    w_scaled = (w_all.astype(jnp.float32) * gain).reshape(blocks * length, channels)
-    w_hi = w_scaled.astype(jnp.bfloat16)
-    w_lo = (w_scaled - w_hi.astype(jnp.float32)).astype(jnp.bfloat16)
-    b_flat = b_all.reshape(blocks * length, local_groups * STATE)
-    c_flat = cconv.reshape(length, local_groups * STATE)
+    w_hi, w_lo = split2(w_all.astype(jnp.float32) * jnp.repeat(gain, HEAD_DIM, axis=1)[:, None, :])
+    w_hi = w_hi.reshape(blocks * length, channels)
+    w_lo = w_lo.reshape(blocks * length, channels)
+    c_flat = cconv.reshape(length, width)
     scores = lax.dot_general(
         c_flat, b_flat, (((1,), (1,)), ((), ())), preferred_element_type=jnp.float32
     )
-    s_hi = scores.astype(jnp.bfloat16)
-    s_lo = (scores - s_hi.astype(jnp.float32)).astype(jnp.bfloat16)
+    s_hi, s_lo = split2(scores)
     carried = (
         jnp.dot(s_hi, w_hi, preferred_element_type=jnp.float32)
         + jnp.dot(s_lo, w_hi, preferred_element_type=jnp.float32)
         + jnp.dot(s_hi, w_lo, preferred_element_type=jnp.float32)
-    ).reshape(length, heads_here, HEAD_DIM)
+    )
+    after = order[:, None] < order[None, :]
+    tail = jnp.exp(jnp.sum(jnp.where(after[:, :, None], lasts[None, :, :], 0.0), axis=1))
+    t_hi, t_lo = split2(w_all.astype(jnp.float32) * jnp.repeat(tail, HEAD_DIM, axis=1)[:, None, :])
+    t_hi = t_hi.reshape(blocks * length, channels)
+    t_lo = t_lo.reshape(blocks * length, channels)
+    contract = (((0,), (0,)), ((), ()))
+    row_state = lax.dot_general(
+        t_hi, b_flat, contract, preferred_element_type=jnp.float32
+    ) + lax.dot_general(t_lo, b_flat, contract, preferred_element_type=jnp.float32)
+    row_decay = jnp.sum(lasts, axis=0)
+    extra = jnp.zeros((8, width), jnp.float32).at[0, :heads_here].set(row_decay)
+    rows_all = lax.all_gather(jnp.concatenate([row_state, extra], 0), "cy")
+    rows = rows_all.shape[0]
+    row = lax.axis_index("cy")
+    states = rows_all[:, :channels]
+    decays = rows_all[:, channels, :heads_here]
+    order_rows = jnp.arange(rows)
+    between_rows = (order_rows[:, None] < order_rows[None, :]) & (order_rows[None, :] < row)
+    span_rows = jnp.sum(jnp.where(between_rows[:, :, None], decays[None, :, :], 0.0), axis=1)
+    gain_rows = jnp.where((order_rows < row)[:, None], jnp.exp(span_rows), 0.0)
+    entering = jnp.sum(states * jnp.repeat(gain_rows, HEAD_DIM, axis=1)[:, :, None], axis=0)
+    before = jnp.sum(jnp.where((order < mine)[:, None], lasts, 0.0), axis=0)
+    entering = entering * jnp.repeat(jnp.exp(before), HEAD_DIM)[:, None]
+    e_hi, e_lo = split2(entering)
+    contract_state = (((1,), (1,)), ((), ()))
+    carried = carried + lax.dot_general(
+        c_flat, e_hi, contract_state, preferred_element_type=jnp.float32
+    ) + lax.dot_general(c_flat, e_lo, contract_state, preferred_element_type=jnp.float32)
+    carried = carried.reshape(length, heads_here, HEAD_DIM)
     carried = carried * jnp.exp(cumulative)[:, :, None]
     ssm_out = inner_out + carried + d_skip[None, :, None] * xconv.astype(jnp.float32)
     gated = ssm_out.reshape(length, channels) * jax.nn.silu(z_in.astype(jnp.float32))
@@ -143,23 +173,29 @@
 
 
 def solution(mesh):
+    grid = mesh.devices
+    inner = 8 if grid.shape[0] % 8 == 0 else 1
+    split = jax.sharding.Mesh(
+        grid.reshape(grid.shape[0] // inner, inner, grid.shape[1]), ("cy", "cz", "tp")
+    )
+    ctx = ("cy", "cz")
     return jax.shard_map(
         local,
-        mesh=mesh,
+        mesh=split,
         in_specs=(
-            P("ctx", "tp"),
-            P("ctx", "tp"),
-            P("ctx", None, None),
-            P("ctx", None, None),
+            P(ctx, "tp"),
+            P(ctx, "tp"),
+            P(ctx, None, None),
+            P(ctx, None, None),
             P(None, "tp"),
             P(),
-            P("ctx", "tp"),
+            P(ctx, "tp"),
             P("tp"),
             P("tp"),
             P("tp"),
             P("tp"),
             P("tp", None),
         ),
-        out_specs=P("ctx", "tp"),
+        out_specs=P(ctx, "tp"),
         check_vma=False,
     )

time: 209 us -> 184 us (0.88)
  waiting for transfers between devices: 112 us -> 66.1 us
  blocking collectives: 36.4 us -> 64.9 us
  other arithmetic: 14.8 us -> 9.2 us
    all_gather x1, waiting for transfers between devices: 110 us -> 64.1 us  [local(): rows_all = lax.all_gather(jnp.concatenate([row_state, extra], 0), 'cy')]
    all_gather x0 -> x1, blocking collectives: none -> 28.5 us  [local(): gathered = lax.all_gather(packet, 'cz')]
    convert_element_type x2, other arithmetic: 5.25 us -> 0.18 us  [the longest x1 0.18 us: split2(): return (hi, (value - hi.astype(jnp.float32)).astype(jnp.bfloat16))]
    mul x1 -> x0, other arithmetic: 3.6 us -> none  [local(): w_all.astype(jnp.float32) * gain]
    reduce_sum x0 -> x3, other arithmetic: none -> 2.75 us  [the longest x1 2.63 us: local(): jnp.sum(states * jnp.repeat(gain_rows, HEAD_DIM, axis=1)[:, :, None], axi...]
  transfers between devices with their start and end apart: 5 -> 5, of which waited for: 3 -> 3; matrix products, arithmetic and copies ran while one was open for 3% -> 4% of each run, Pallas kernels for 0% -> 0%
where the time goes in v4:
time: 184 us; the launch traced here: 183 us
  waiting for transfers between devices  66.1 us (36%)
  blocking collectives  64.9 us (35%)
  starting transfers between devices  16.4 us (9%)
  between operations  13.8 us (8%)
  other arithmetic  9.2 us (5%)
  matrix products  7.49 us (4%)
  local copies, waits for them, and re-layouts  5.13 us (3%)
    all_gather x1, waiting for transfers between devices, local(): rows_all = lax.all_gather(jnp.concatenate([row_state, extra], 0), 'cy')  64.1 us
    all_to_all x1, blocking collectives, local(): received = lax.all_to_all(pieces_out, 'tp', 0, 0, tiled=True)  36.4 us
    all_gather x1, blocking collectives, local(): gathered = lax.all_gather(packet, 'cz')  28.5 us
    ppermute x2, starting transfers between devices, shifted(): return lax.ppermute(block, axis, route)  10.6 us
    ppermute x2, starting transfers between devices, group_sum(): total = total + lax.ppermute(total, axis, route)  5.82 us
    dot_general x1, matrix products, local(): partial_out = jnp.dot(hidden, w_out, preferred_element_type=jnp.float32)  5.01 us
  transfers between devices with their start and end apart: 5, of which 3 were waited for; matrix products, arithmetic and copies ran while one was open for 4% of the time, Pallas kernels for 0%

profile of v4, /device:TPU:1, one launch (start us, length us, event | category | flops | bytes accessed | tf_op | source)
XLA Modules:
  0.0 183.1 jit_solution(5750379696562603676)
XLA Ops:
  6.5 1.1 constant_dynamic-slice_fusion
  7.7 5.7 %collective-permute-start.1 = (bf16[3,512]{1,0:T(4,128)(2,1)S(1)}, bf16[3,512]{1,0:T(4,128)(2,1)S(1)}, u32[]{:S(2)}, u32[]{:S(2)}) collective-permute-start(bf16[3,512]{1,0:T(4,128)(2,1)S(1)} %pad_maximum_fusion.1), channel_id=1, source_target_pairs={{0,16},{16,32},{32,48},{48,64},{64,80},{80,96},{96,112},{112,128},... | collective-permute-start | bytes 9224 | tf_op jit(solution)/shard_map/ppermute | solution.py:17
  13.4 0.7 slice.130
  14.1 4.9 %collective-permute-start = (bf16[3,512]{1,0:T(4,128)(2,1)S(1)}, bf16[3,512]{1,0:T(4,128)(2,1)S(1)}, u32[]{:S(2)}, u32[]{:S(2)}) collective-permute-start(bf16[3,512]{1,0:T(4,128)(2,1)S(1)} %slice.130), channel_id=1, source_target_pairs={{0,16},{16,32},{32,48},{48,64},{64,80},{80,96},{96,112},{112,128},... | collective-permute-start | bytes 9224 | tf_op jit(solution)/shard_map/ppermute | solution.py:17
  19.0 0.7 neg.20
  19.7 0.8 broadcast_multiply_fusion
  20.7 0.7 dynamic-slice_convert_fusion
  21.5 0.8 fusion.70
  22.4 0.8 fusion.63
  23.7 0.9 maximum_convert_fusion
  24.6 28.5 %all-gather = bf16[512,896]{1,0:T(8,128)(2,1)S(1)} all-gather(bf16[64,896]{1,0:T(8,128)(2,1)S(1)} %pad_maximum_fusion), channel_id=2, replica_groups=mesh['cy'=8,'cz'=8,'tp'=16] {'cz'}, dimensions={0}, use_global_device_ids=true | all-gather | bytes 1032192 | tf_op jit(solution)/shard_map/all_gather | solution.py:100
  53.5 0.4 convolution_bitcast_fusion
  53.9 0.3 fusion.5
  54.2 0.9 select_maximum_fusion
  56.0 0.2 fusion.46
  56.2 0.2 fusion.11
  56.4 0.2 fusion.59
  56.6 0.2 convolution_add_fusion.1
  56.8 64.1 %all-gather.4.cloned.1.call-done = f32[4160,256]{1,0:T(8,128)} async-done(((f32[520,256]{1,0:T(8,128)}), f32[4160,256]{1,0:T(8,128)}) %all-gather.4.cloned.1.call-update) | async-done | bytes 4259856 | tf_op jit(solution)/shard_map/all_gather | solution.py:135
  120.9 0.8 slice.185
  122.0 2.6 %fusion = f32[512,256]{1,0:T(8,128)S(1)} fusion(f32[8,520,256]{2,1,0:T(8,128)} %bitcast.66, f32[8,512]{1,0:T(8,128)S(1)} %mul.250), kind=kLoop, calls=%fused_computation.2 | loop fusion | flops 1966080 | bytes 4734976 | tf_op jit(solution)/shard_map/reduce_sum | solution.py:144
  124.6 0.3 fusion.16
  124.9 0.3 fusion.19
  125.1 0.2 fusion.9
  125.5 0.3 fusion.7
  126.1 2.7 %collective-permute-start.2 = (f32[64,1]{0,1:T(1,128)S(1)}, f32[64,1]{0,1:T(1,128)S(1)}, u32[]{:S(2)}, u32[]{:S(2)}) collective-permute-start(f32[64,1]{0,1:T(1,128)S(1)} %bitcast.94), channel_id=1, source_target_pairs={{0,1},{1,0},{2,3},{3,2},{4,5},{5,4},{6,7},{7,6},{8,9},{9,8},{10,11... | collective-permute-start | bytes 776 | tf_op jit(solution)/shard_map/ppermute | solution.py:25
  128.8 0.8 collective-permute-done.2
  129.6 3.1 %collective-permute-start.3 = (f32[64,1]{0,1:T(1,128)S(1)}, f32[64,1]{0,1:T(1,128)S(1)}, u32[]{:S(2)}, u32[]{:S(2)}) collective-permute-start(f32[64,1]{0,1:T(1,128)S(1)} %bitcast_add_fusion), channel_id=1, source_target_pairs={{0,2},{1,3},{2,0},{3,1},{4,6},{5,7},{6,4},{7,5},{8,10},{9,11},{10,... | collective-permute-start | bytes 776 | tf_op jit(solution)/shard_map/ppermute | solution.py:25
  132.7 1.2 collective-permute-done.3
  133.9 5.0 %convolution_convert_fusion = bf16[64,8192]{1,0:T(8,128)(2,1)S(1)} fusion(bf16[512,8192]{1,0:T(8,128)(2,1)} %param.27, f32[512]{0:T(512)S(1)} %copy-done.1, f32[64]{0:T(128)S(1)} %rsqrt_bitcast_fusion, f32[64,512]{1,0:T(8,128)S(1)} %copy.68, bf16[64,512]{1,0:T(8,128)(2,1)S(1)} %copy-done), kind=kOutput, calls=%fused_computation | convolution fusion | flops 537690112 | bytes 9636096 | tf_op jit(solution)/shard_map/dot_general | solution.py:167
  139.1 36.4 %all_to_all.5 = bf16[16,64,512]{2,1,0:T(8,128)(2,1)S(1)} all-to-all(bf16[16,64,512]{2,1,0:T(8,128)(2,1)S(1)} %bitcast.64), channel_id=1, replica_groups=mesh['cy'=8,'cz'=8,'tp'=16] {'tp'}, dimensions={0} | all-to-all | bytes 2097152 | tf_op jit(solution)/shard_map/all_to_all | solution.py:170
  175.5 0.8 reduce_sum.85
  (61 shorter events, 2.8 us)
Async XLA Ops:
  6.5 114.3 %all-gather.4.cloned.1.call-start = ((), (), s32[]{:S(2)}) async-start(), calls=%async_computation.1 | async-start | bytes 4792320 | tf_op jit(solution)/shard_map/all_gather | solution.py:135
  7.7 15.8 %collective-permute-start.1 = (bf16[3,512]{1,0:T(4,128)(2,1)S(1)}, bf16[3,512]{1,0:T(4,128)(2,1)S(1)}, u32[]{:S(2)}, u32[]{:S(2)}) collective-permute-start(bf16[3,512]{1,0:T(4,128)(2,1)S(1)} %pad_maximum_fusion.1), channel_id=1, source_target_pairs={{0,16},{16,32},{32,48},{48,64},{64,80},{80,96},{96,112},{112,128},... | collective-permute-start | bytes 9224 | tf_op jit(solution)/shard_map/ppermute | solution.py:17
  14.1 9.5 %collective-permute-start = (bf16[3,512]{1,0:T(4,128)(2,1)S(1)}, bf16[3,512]{1,0:T(4,128)(2,1)S(1)}, u32[]{:S(2)}, u32[]{:S(2)}) collective-permute-start(bf16[3,512]{1,0:T(4,128)(2,1)S(1)} %slice.130), channel_id=1, source_target_pairs={{0,16},{16,32},{32,48},{48,64},{64,80},{80,96},{96,112},{112,128},... | collective-permute-start | bytes 9224 | tf_op jit(solution)/shard_map/ppermute | solution.py:17
  56.6 68.9 %copy-start.2 = (f32[8]{0:T(128)S(1)}, f32[8]{0:T(128)}, u32[]{:S(2)}) copy-start(f32[8]{0:T(128)} %param.25) | copy-start | bytes 100
  121.9 4.0 %copy-start = (bf16[64,512]{1,0:T(8,128)(2,1)S(1)}, bf16[64,512]{1,0:T(8,128)(2,1)}, u32[]{:S(2)}) copy-start(bf16[64,512]{1,0:T(8,128)(2,1)} %param.17) | copy-start | bytes 196612
  122.0 12.0 %copy-start.1 = (f32[512]{0:T(512)S(1)}, f32[512]{0:T(512)}, u32[]{:S(2)}) copy-start(f32[512]{0:T(512)} %param.26) | copy-start | bytes 6148
  126.1 3.5 %collective-permute-start.2 = (f32[64,1]{0,1:T(1,128)S(1)}, f32[64,1]{0,1:T(1,128)S(1)}, u32[]{:S(2)}, u32[]{:S(2)}) collective-permute-start(f32[64,1]{0,1:T(1,128)S(1)} %bitcast.94), channel_id=1, source_target_pairs={{0,1},{1,0},{2,3},{3,2},{4,5},{5,4},{6,7},{7,6},{8,9},{9,8},{10,11... | collective-permute-start | bytes 776 | tf_op jit(solution)/shard_map/ppermute | solution.py:25
  129.6 4.3 %collective-permute-start.3 = (f32[64,1]{0,1:T(1,128)S(1)}, f32[64,1]{0,1:T(1,128)S(1)}, u32[]{:S(2)}, u32[]{:S(2)}) collective-permute-start(f32[64,1]{0,1:T(1,128)S(1)} %bitcast_add_fusion), channel_id=1, source_target_pairs={{0,2},{1,3},{2,0},{3,1},{4,6},{5,7},{6,4},{7,5},{8,10},{9,11},{10,... | collective-permute-start | bytes 776 | tf_op jit(solution)/shard_map/ppermute | solution.py:25
Sparse Core Ops, SparseCore 0:
  55.2 65.6 all-gather.3

commit v5 on v4

--- a/solution.py
+++ b/solution.py
@@ -154,21 +154,26 @@
     ssm_out = inner_out + carried + d_skip[None, :, None] * xconv.astype(jnp.float32)
     gated = ssm_out.reshape(length, channels) * jax.nn.silu(z_in.astype(jnp.float32))
     norm_size = per_group * HEAD_DIM
-    grouped = gated.reshape(length, local_groups, channels // local_groups)
-    partial_squares = jnp.sum(grouped * grouped, axis=-1)
-    if local_groups == 1:
-        squares = group_sum(partial_squares, "tp", per_group // heads_here)
-    else:
-        squares = partial_squares
-    scale = lax.rsqrt(squares / norm_size + 1e-05)
-    hidden = ((grouped * scale[:, :, None]).reshape(length, channels) * norm_gain[None, :]).astype(
-        jnp.bfloat16
-    )
-    partial_out = jnp.dot(hidden, w_out, preferred_element_type=jnp.float32)
-    owners = lax.axis_size("tp")
+    owners = lax.psum(1, "tp")
+    span_tp = per_group // heads_here
+    partial_squares = jnp.sum(gated * gated, axis=-1)
+    unscaled = (gated * norm_gain[None, :]).astype(jnp.bfloat16)
+    partial_out = jnp.dot(unscaled, w_out, preferred_element_type=jnp.float32)
     pieces_out = partial_out.astype(jnp.bfloat16).reshape(length, owners, -1).transpose(1, 0, 2)
-    received = lax.all_to_all(pieces_out, "tp", 0, 0, tiled=True)
-    summed = jnp.sum(received.astype(jnp.float32), axis=0).astype(jnp.bfloat16)
+    sq_block = jnp.zeros((length, SIDE), jnp.bfloat16)
+    sq_block = sq_block.at[:, 0:3].set(jnp.stack(split3(partial_squares), axis=1))
+    send = jnp.concatenate(
+        [pieces_out, jnp.broadcast_to(sq_block[None], (owners, length, SIDE))], axis=2
+    )
+    received = lax.all_to_all(send, "tp", 0, 0, tiled=True)
+    cols = pieces_out.shape[2]
+    parts = received[:, :, :cols].astype(jnp.float32)
+    sq = received[:, :, cols : cols + 3].astype(jnp.float32)
+    src_squares = sq[:, :, 0] + sq[:, :, 1] + sq[:, :, 2]
+    group_squares = jnp.sum(src_squares.reshape(owners // span_tp, span_tp, length), axis=1)
+    scale = lax.rsqrt(group_squares / norm_size + 1e-05)
+    scale_src = jnp.repeat(scale, span_tp, axis=0)
+    summed = jnp.sum(parts * scale_src[:, :, None], axis=0).astype(jnp.bfloat16)
     return summed
 
 

time: 184 us -> 182 us (0.989)
  starting transfers between devices: 16.4 us -> 10.6 us
  blocking collectives: 64.9 us -> 69.9 us
  waiting for transfers between devices: 66.1 us -> 63.5 us
    ppermute x2 -> x0, starting transfers between devices: 5.82 us -> none  [group_sum(): total = total + lax.ppermute(total, axis, route)]
    all_to_all x1, blocking collectives: 36.4 us -> 41.4 us  [local(): received = lax.all_to_all(send, 'tp', 0, 0, tiled=True)]
    ppermute x2 -> x0, waiting for transfers between devices: 2.01 us -> none  [group_sum(): total = total + lax.ppermute(total, axis, route)]
  transfers between devices with their start and end apart: 5 -> 3, of which waited for: 3 -> 1; matrix products, arithmetic and copies ran while one was open for 4% -> 4% of each run, Pallas kernels for 0% -> 0%
where the time goes in v5:
time: 182 us
  blocking collectives  69.9 us (38%)
  waiting for transfers between devices  63.5 us (35%)
  between operations  13.8 us (8%)
  other arithmetic  10.8 us (6%)
  starting transfers between devices  10.6 us (6%)
  matrix products  7.43 us (4%)
  local copies, waits for them, and re-layouts  5.54 us (3%)
    all_gather x1, waiting for transfers between devices, local(): rows_all = lax.all_gather(jnp.concatenate([row_state, extra], 0), 'cy')  63.4 us
    all_to_all x1, blocking collectives, local(): received = lax.all_to_all(send, 'tp', 0, 0, tiled=True)  41.4 us
    all_gather x1, blocking collectives, local(): gathered = lax.all_gather(packet, 'cz')  28.5 us
    ppermute x2, starting transfers between devices, shifted(): return lax.ppermute(block, axis, route)  10.6 us
    dot_general x1, matrix products, local(): partial_out = jnp.dot(unscaled, w_out, preferred_element_type=jnp.float32)  4.94 us
  transfers between devices with their start and end apart: 3, of which 1 were waited for; matrix products, arithmetic and copies ran while one was open for 4% of the time, Pallas kernels for 0%

profile of v5, /device:TPU:1, one launch (start us, length us, event | category | flops | bytes accessed | tf_op | source)
XLA Modules:
  0.0 181.6 jit_solution(18327987882343795971)
XLA Ops:
  6.5 1.1 constant_dynamic-slice_fusion
  7.7 5.7 %collective-permute-start.1 = (bf16[3,512]{1,0:T(4,128)(2,1)S(1)}, bf16[3,512]{1,0:T(4,128)(2,1)S(1)}, u32[]{:S(2)}, u32[]{:S(2)}) collective-permute-start(bf16[3,512]{1,0:T(4,128)(2,1)S(1)} %pad_maximum_fusion.2), channel_id=1, source_target_pairs={{0,16},{16,32},{32,48},{48,64},{64,80},{80,96},{96,112},{112,128},... | collective-permute-start | bytes 9224 | tf_op jit(solution)/shard_map/ppermute | solution.py:17
  13.4 0.7 slice.161
  14.1 4.9 %collective-permute-start = (bf16[3,512]{1,0:T(4,128)(2,1)S(1)}, bf16[3,512]{1,0:T(4,128)(2,1)S(1)}, u32[]{:S(2)}, u32[]{:S(2)}) collective-permute-start(bf16[3,512]{1,0:T(4,128)(2,1)S(1)} %slice.161), channel_id=1, source_target_pairs={{0,16},{16,32},{32,48},{48,64},{64,80},{80,96},{96,112},{112,128},... | collective-permute-start | bytes 9224 | tf_op jit(solution)/shard_map/ppermute | solution.py:17
  19.0 0.7 neg.20
  19.7 0.8 broadcast_multiply_fusion
  20.7 0.7 dynamic-slice_convert_fusion
  21.5 0.8 fusion.70
  22.4 0.8 fusion.63
  23.7 0.9 maximum_convert_fusion
  24.6 28.5 %all-gather = bf16[512,896]{1,0:T(8,128)(2,1)S(1)} all-gather(bf16[64,896]{1,0:T(8,128)(2,1)S(1)} %pad_maximum_fusion.1), channel_id=2, replica_groups=mesh['cy'=8,'cz'=8,'tp'=16] {'cz'}, dimensions={0}, use_global_device_ids=true | all-gather | bytes 1032192 | tf_op jit(solution)/shard_map/all_gather | solution.py:100
  53.5 0.4 convolution_bitcast_fusion
  53.9 0.3 fusion.5
  54.2 0.9 select_maximum_fusion
  55.2 0.7 compare_reduce_fusion
  56.6 0.2 fusion.45
  56.8 0.2 fusion.11
  57.0 0.2 fusion.59
  57.2 0.2 convolution_add_fusion.1
  57.4 63.4 %all-gather.4.cloned.1.call-done = f32[4160,256]{1,0:T(8,128)} async-done(((f32[520,256]{1,0:T(8,128)}), f32[4160,256]{1,0:T(8,128)}) %all-gather.4.cloned.1.call-update) | async-done | bytes 4259856 | tf_op jit(solution)/shard_map/all_gather | solution.py:135
  120.9 0.8 slice.221
  121.9 2.6 %fusion = f32[512,256]{1,0:T(8,128)S(1)} fusion(f32[8,520,256]{2,1,0:T(8,128)} %bitcast.77, f32[8,512]{1,0:T(8,128)S(1)} %mul.248), kind=kLoop, calls=%fused_computation.2 | loop fusion | flops 1966080 | bytes 4734976 | tf_op jit(solution)/shard_map/reduce_sum | solution.py:144
  124.6 0.3 fusion.16
  124.9 0.3 fusion.19
  125.1 0.2 fusion.9
  125.5 0.3 fusion.7
  125.9 0.2 multiply_reduce_fusion.1
  126.1 4.9 %convolution_convert_fusion = bf16[64,8192]{1,0:T(8,128)(2,1)S(1)} fusion(bf16[512,8192]{1,0:T(8,128)(2,1)} %param.29, f32[512]{0:T(512)S(1)} %copy-done.1, f32[64,512]{1,0:T(8,128)S(1)} %copy.78, bf16[64,512]{1,0:T(8,128)(2,1)S(1)} %copy-done), kind=kOutput, calls=%fused_computation | convolution fusion | flops 537657344 | bytes 9635840 | tf_op jit(solution)/shard_map/dot_general | solution.py:161
  131.2 0.7 maximum_select_fusion
  132.1 41.4 %all_to_all.5 = bf16[16,64,640]{2,1,0:T(8,128)(2,1)S(1)} all-to-all(bf16[16,64,640]{2,1,0:T(8,128)(2,1)S(1)} %pad_maximum_fusion), channel_id=1, replica_groups=mesh['cy'=8,'cz'=8,'tp'=16] {'tp'}, dimensions={0} | all-to-all | bytes 2621440 | tf_op jit(solution)/shard_map/all_to_all | solution.py:168
  173.6 0.2 copy.88
  173.8 0.9 multiply_reduce_fusion
  (70 shorter events, 3.0 us)
Async XLA Ops:
  6.5 114.3 %all-gather.4.cloned.1.call-start = ((), (), s32[]{:S(2)}) async-start(), calls=%async_computation.1 | async-start | bytes 4792320 | tf_op jit(solution)/shard_map/all_gather | solution.py:135
  7.7 15.8 %collective-permute-start.1 = (bf16[3,512]{1,0:T(4,128)(2,1)S(1)}, bf16[3,512]{1,0:T(4,128)(2,1)S(1)}, u32[]{:S(2)}, u32[]{:S(2)}) collective-permute-start(bf16[3,512]{1,0:T(4,128)(2,1)S(1)} %pad_maximum_fusion.2), channel_id=1, source_target_pairs={{0,16},{16,32},{32,48},{48,64},{64,80},{80,96},{96,112},{112,128},... | collective-permute-start | bytes 9224 | tf_op jit(solution)/shard_map/ppermute | solution.py:17
  14.1 9.5 %collective-permute-start = (bf16[3,512]{1,0:T(4,128)(2,1)S(1)}, bf16[3,512]{1,0:T(4,128)(2,1)S(1)}, u32[]{:S(2)}, u32[]{:S(2)}) collective-permute-start(bf16[3,512]{1,0:T(4,128)(2,1)S(1)} %slice.161), channel_id=1, source_target_pairs={{0,16},{16,32},{32,48},{48,64},{64,80},{80,96},{96,112},{112,128},... | collective-permute-start | bytes 9224 | tf_op jit(solution)/shard_map/ppermute | solution.py:17
  124.6 0.9 copy-start.2
  124.6 1.4 copy-start
  124.6 1.5 copy-start.1
Sparse Core Ops, SparseCore 0:
  55.2 65.5 all-gather.3

commit v6 on v5

--- a/solution.py
+++ b/solution.py
@@ -160,16 +160,17 @@
     unscaled = (gated * norm_gain[None, :]).astype(jnp.bfloat16)
     partial_out = jnp.dot(unscaled, w_out, preferred_element_type=jnp.float32)
     pieces_out = partial_out.astype(jnp.bfloat16).reshape(length, owners, -1).transpose(1, 0, 2)
-    sq_block = jnp.zeros((length, SIDE), jnp.bfloat16)
-    sq_block = sq_block.at[:, 0:3].set(jnp.stack(split3(partial_squares), axis=1))
+    cols = pieces_out.shape[2]
+    sq_row = jnp.zeros((cols,), jnp.bfloat16).at[: 3 * length].set(
+        jnp.concatenate(split3(partial_squares))
+    )
     send = jnp.concatenate(
-        [pieces_out, jnp.broadcast_to(sq_block[None], (owners, length, SIDE))], axis=2
+        [pieces_out, jnp.broadcast_to(sq_row[None, None], (owners, 1, cols))], axis=1
     )
     received = lax.all_to_all(send, "tp", 0, 0, tiled=True)
-    cols = pieces_out.shape[2]
-    parts = received[:, :, :cols].astype(jnp.float32)
-    sq = received[:, :, cols : cols + 3].astype(jnp.float32)
-    src_squares = sq[:, :, 0] + sq[:, :, 1] + sq[:, :, 2]
+    parts = received[:, :length].astype(jnp.float32)
+    sq = received[:, length, : 3 * length].astype(jnp.float32)
+    src_squares = sq[:, :length] + sq[:, length : 2 * length] + sq[:, 2 * length :]
     group_squares = jnp.sum(src_squares.reshape(owners // span_tp, span_tp, length), axis=1)
     scale = lax.rsqrt(group_squares / norm_size + 1e-05)
     scale_src = jnp.repeat(scale, span_tp, axis=0)

time: 182 us -> 178 us (0.978)
  blocking collectives: 69.9 us -> 67.3 us
  other arithmetic: 10.8 us -> 8.8 us
    all_to_all x1, blocking collectives: 41.4 us -> 38.7 us  [local(): received = lax.all_to_all(send, 'tp', 0, 0, tiled=True)]
where the time goes in v6:
time: 178 us; the launch traced here: 177 us
  blocking collectives  67.3 us (38%)
  waiting for transfers between devices  64.1 us (36%)
  between operations  13.8 us (8%)
  starting transfers between devices  10.6 us (6%)
  other arithmetic  8.8 us (5%)
  matrix products  7.41 us (4%)
  local copies, waits for them, and re-layouts  5.22 us (3%)
    all_gather x1, waiting for transfers between devices, local(): rows_all = lax.all_gather(jnp.concatenate([row_state, extra], 0), 'cy')  64.1 us
    all_to_all x1, blocking collectives, local(): received = lax.all_to_all(send, 'tp', 0, 0, tiled=True)  38.7 us
    all_gather x1, blocking collectives, local(): gathered = lax.all_gather(packet, 'cz')  28.5 us
    ppermute x2, starting transfers between devices, shifted(): return lax.ppermute(block, axis, route)  10.6 us
    dot_general x1, matrix products, local(): partial_out = jnp.dot(unscaled, w_out, preferred_element_type=jnp.float32)  4.94 us
  transfers between devices with their start and end apart: 3, of which 1 were waited for; matrix products, arithmetic and copies ran while one was open for 4% of the time, Pallas kernels for 0%

profile of v6, /device:TPU:1, one launch (start us, length us, event | category | flops | bytes accessed | tf_op | source)
XLA Modules:
  0.0 177.3 jit_solution(13290169319581413222)
XLA Ops:
  6.5 1.1 constant_dynamic-slice_fusion
  7.7 5.7 %collective-permute-start.1 = (bf16[3,512]{1,0:T(4,128)(2,1)S(1)}, bf16[3,512]{1,0:T(4,128)(2,1)S(1)}, u32[]{:S(2)}, u32[]{:S(2)}) collective-permute-start(bf16[3,512]{1,0:T(4,128)(2,1)S(1)} %pad_maximum_fusion.2), channel_id=1, source_target_pairs={{0,16},{16,32},{32,48},{48,64},{64,80},{80,96},{96,112},{112,128},... | collective-permute-start | bytes 9224 | tf_op jit(solution)/shard_map/ppermute | solution.py:17
  13.5 0.7 slice.156
  14.2 4.9 %collective-permute-start = (bf16[3,512]{1,0:T(4,128)(2,1)S(1)}, bf16[3,512]{1,0:T(4,128)(2,1)S(1)}, u32[]{:S(2)}, u32[]{:S(2)}) collective-permute-start(bf16[3,512]{1,0:T(4,128)(2,1)S(1)} %slice.156), channel_id=1, source_target_pairs={{0,16},{16,32},{32,48},{48,64},{64,80},{80,96},{96,112},{112,128},... | collective-permute-start | bytes 9224 | tf_op jit(solution)/shard_map/ppermute | solution.py:17
  19.1 0.7 neg.20
  19.7 0.8 broadcast_multiply_fusion
  20.8 0.7 dynamic-slice_convert_fusion
  21.5 0.8 fusion.75
  22.4 0.8 fusion.68
  23.3 0.1 mul.239
  23.9 28.5 %all-gather = bf16[512,896]{1,0:T(8,128)(2,1)S(1)} all-gather(bf16[64,896]{1,0:T(8,128)(2,1)S(1)} %pad_maximum_fusion.1), channel_id=2, replica_groups=mesh['cy'=8,'cz'=8,'tp'=16] {'cz'}, dimensions={0}, use_global_device_ids=true | all-gather | bytes 1032192 | tf_op jit(solution)/shard_map/all_gather | solution.py:100
  52.7 0.3 convolution_bitcast_fusion
  53.0 0.3 fusion.5
  53.4 0.9 select_maximum_fusion
  54.9 0.1 copy.58
  55.0 0.1 fusion.47
  55.2 0.2 fusion.45
  55.4 0.2 fusion.11
  55.6 0.2 fusion.64
  55.8 0.2 convolution_add_fusion.1
  56.0 64.1 %all-gather.4.cloned.1.call-done = f32[4160,256]{1,0:T(8,128)} async-done(((f32[520,256]{1,0:T(8,128)}), f32[4160,256]{1,0:T(8,128)}) %all-gather.4.cloned.1.call-update) | async-done | bytes 4259856 | tf_op jit(solution)/shard_map/all_gather | solution.py:135
  120.1 0.8 slice.216
  121.2 2.6 %fusion = f32[512,256]{1,0:T(8,128)S(1)} fusion(f32[8,520,256]{2,1,0:T(8,128)} %bitcast.67, f32[8,512]{1,0:T(8,128)S(1)} %mul.248), kind=kLoop, calls=%fused_computation.2 | loop fusion | flops 1966080 | bytes 4734976 | tf_op jit(solution)/shard_map/reduce_sum | solution.py:144
  123.8 0.3 fusion.16
  124.1 0.3 fusion.19
  124.4 0.2 fusion.9
  124.6 0.1 copy.67
  124.7 0.3 fusion.7
  125.2 0.2 multiply_reduce_fusion.1
  125.3 4.9 %convolution_convert_fusion = bf16[64,8192]{1,0:T(8,128)(2,1)S(1)} fusion(bf16[512,8192]{1,0:T(8,128)(2,1)} %param.29, f32[512]{0:T(512)S(1)} %copy-done.2, f32[64,512]{1,0:T(8,128)S(1)} %copy.69, bf16[64,512]{1,0:T(8,128)(2,1)S(1)} %copy-done), kind=kOutput, calls=%fused_computation | convolution fusion | flops 537657344 | bytes 9635840 | tf_op jit(solution)/shard_map/dot_general | solution.py:161
  130.6 38.7 %all_to_all.5 = bf16[16,65,512]{2,1,0:T(8,128)(2,1)S(1)} all-to-all(bf16[16,65,512]{2,1,0:T(8,128)(2,1)S(1)} %pad_maximum_fusion), channel_id=1, replica_groups=mesh['cy'=8,'cz'=8,'tp'=16] {'tp'}, dimensions={0} | all-to-all | bytes 2129920 | tf_op jit(solution)/shard_map/all_to_all | solution.py:170
  169.5 0.9 multiply_reduce_fusion
  (67 shorter events, 2.6 us)
Async XLA Ops:
  6.5 17.2 %copy-start.1 = (bf16[64,512]{1,0:T(8,128)(2,1)S(1)}, bf16[64,512]{1,0:T(8,128)(2,1)}, u32[]{:S(2)}) copy-start(bf16[64,512]{1,0:T(8,128)(2,1)} %param.18) | copy-start | bytes 196612
  6.5 113.5 %all-gather.4.cloned.1.call-start = ((), (), s32[]{:S(2)}) async-start(), calls=%async_computation.1 | async-start | bytes 4792320 | tf_op jit(solution)/shard_map/all_gather | solution.py:135
  7.7 15.8 %collective-permute-start.1 = (bf16[3,512]{1,0:T(4,128)(2,1)S(1)}, bf16[3,512]{1,0:T(4,128)(2,1)S(1)}, u32[]{:S(2)}, u32[]{:S(2)}) collective-permute-start(bf16[3,512]{1,0:T(4,128)(2,1)S(1)} %pad_maximum_fusion.2), channel_id=1, source_target_pairs={{0,16},{16,32},{32,48},{48,64},{64,80},{80,96},{96,112},{112,128},... | collective-permute-start | bytes 9224 | tf_op jit(solution)/shard_map/ppermute | solution.py:17
  14.2 9.5 %collective-permute-start = (bf16[3,512]{1,0:T(4,128)(2,1)S(1)}, bf16[3,512]{1,0:T(4,128)(2,1)S(1)}, u32[]{:S(2)}, u32[]{:S(2)}) collective-permute-start(bf16[3,512]{1,0:T(4,128)(2,1)S(1)} %slice.156), channel_id=1, source_target_pairs={{0,16},{16,32},{32,48},{48,64},{64,80},{80,96},{96,112},{112,128},... | collective-permute-start | bytes 9224 | tf_op jit(solution)/shard_map/ppermute | solution.py:17
  123.8 0.9 copy-start.3
  123.8 1.3 copy-start
  123.8 1.5 copy-start.2
Sparse Core Ops, SparseCore 0:
  54.4 65.6 all-gather.3

commit v7 on v6

--- a/solution.py
+++ b/solution.py
@@ -91,18 +91,20 @@
     weighted = (tail_weight[:, :, None] * xconv.astype(jnp.float32)).astype(jnp.bfloat16)
 
     cum_last = cumulative[-1]
-    side = jnp.zeros((length, SIDE), jnp.bfloat16)
-    side = side.at[0:3, 0:heads_here].set(jnp.stack(split3(cum_last)))
     width = local_groups * STATE
+    side = jnp.zeros((channels + width,), jnp.bfloat16)
+    side = side.at[: 3 * heads_here].set(jnp.concatenate(split3(cum_last)))
     packet = jnp.concatenate(
-        [weighted.reshape(length, channels), bconv.reshape(length, width), side], 1
-    )
+        [weighted.reshape(length, channels), bconv.reshape(length, width)], 1
+    )
+    packet = jnp.concatenate([packet, side[None]], 0)
     gathered = lax.all_gather(packet, "cz")
     blocks = gathered.shape[0]
     mine = lax.axis_index("cz")
-    w_all = gathered[:, :, :channels]
-    b_flat = gathered[:, :, channels : channels + width].reshape(blocks * length, width)
-    pieces = gathered[:, 0:3, channels + width :][:, :, :heads_here].astype(jnp.float32)
+    w_all = gathered[:, :length, :channels]
+    b_flat = gathered[:, :length, channels : channels + width].reshape(blocks * length, width)
+    pieces = gathered[:, length, : 3 * heads_here].astype(jnp.float32)
+    pieces = pieces.reshape(blocks, 3, heads_here)
     lasts = pieces[:, 0] + pieces[:, 1] + pieces[:, 2]
     order = jnp.arange(blocks)
     between = (order[:, None] < order[None, :]) & (order[None, :] < mine)

time: 178 us -> 178 us (level)
  no operation moved by 1% of the time
where the time goes in v7:
time: 178 us; the launch traced here: 177 us
  blocking collectives  67.2 us (38%)
  waiting for transfers between devices  64.1 us (36%)
  between operations  13.8 us (8%)
  starting transfers between devices  10.6 us (6%)
  other arithmetic  8.87 us (5%)
  matrix products  7.41 us (4%)
  local copies, waits for them, and re-layouts  5.31 us (3%)
    all_gather x1, waiting for transfers between devices, local(): rows_all = lax.all_gather(jnp.concatenate([row_state, extra], 0), 'cy')  64.1 us
    all_to_all x1, blocking collectives, local(): received = lax.all_to_all(send, 'tp', 0, 0, tiled=True)  38.7 us
    all_gather x1, blocking collectives, local(): gathered = lax.all_gather(packet, 'cz')  28.4 us
    ppermute x2, starting transfers between devices, shifted(): return lax.ppermute(block, axis, route)  10.6 us
    dot_general x1, matrix products, local(): partial_out = jnp.dot(unscaled, w_out, preferred_element_type=jnp.float32)  4.94 us
  transfers between devices with their start and end apart: 3, of which 1 were waited for; matrix products, arithmetic and copies ran while one was open for 4% of the time, Pallas kernels for 0%

profile of v7, /device:TPU:1, one launch (start us, length us, event | category | flops | bytes accessed | tf_op | source)
XLA Modules:
  0.0 177.3 jit_solution(18429150840192786803)
XLA Ops:
  6.5 1.1 constant_dynamic-slice_fusion
  7.7 5.7 %collective-permute-start.1 = (bf16[3,512]{1,0:T(4,128)(2,1)S(1)}, bf16[3,512]{1,0:T(4,128)(2,1)S(1)}, u32[]{:S(2)}, u32[]{:S(2)}) collective-permute-start(bf16[3,512]{1,0:T(4,128)(2,1)S(1)} %pad_maximum_fusion.1), channel_id=1, source_target_pairs={{0,16},{16,32},{32,48},{48,64},{64,80},{80,96},{96,112},{112,128},... | collective-permute-start | bytes 9224 | tf_op jit(solution)/shard_map/ppermute | solution.py:17
  13.5 0.7 slice.145
  14.2 4.9 %collective-permute-start = (bf16[3,512]{1,0:T(4,128)(2,1)S(1)}, bf16[3,512]{1,0:T(4,128)(2,1)S(1)}, u32[]{:S(2)}, u32[]{:S(2)}) collective-permute-start(bf16[3,512]{1,0:T(4,128)(2,1)S(1)} %slice.145), channel_id=1, source_target_pairs={{0,16},{16,32},{32,48},{48,64},{64,80},{80,96},{96,112},{112,128},... | collective-permute-start | bytes 9224 | tf_op jit(solution)/shard_map/ppermute | solution.py:17
  19.1 0.7 neg.20
  19.7 0.8 broadcast_multiply_fusion
  20.8 0.7 dynamic-slice_convert_fusion
  21.5 0.8 fusion.71
  22.4 0.8 fusion.64
  23.3 0.1 mul.239
  23.9 28.4 %all-gather.2 = bf16[8,65,768]{2,1,0:T(8,128)(2,1)S(1)} all-gather(bf16[1,65,768]{2,1,0:T(8,128)(2,1)S(1)} %fusion.40), channel_id=2, replica_groups=mesh['cy'=8,'cz'=8,'tp'=16] {'cz'}, dimensions={0}, use_global_device_ids=true | all-gather | bytes 898560 | tf_op jit(solution)/shard_map/all_gather | solution.py:101
  52.8 0.4 convolution_bitcast_fusion
  53.1 0.3 fusion.5
  53.5 0.9 select_maximum_fusion
  55.0 0.1 copy.61
  55.1 0.1 fusion.46
  55.2 0.2 fusion.44
  55.5 0.2 fusion.11
  55.6 0.2 fusion.60
  55.8 0.2 convolution_add_fusion.1
  56.1 64.1 %all-gather.5.cloned.1.call-done = f32[4160,256]{1,0:T(8,128)} async-done(((f32[520,256]{1,0:T(8,128)}), f32[4160,256]{1,0:T(8,128)}) %all-gather.5.cloned.1.call-update) | async-done | bytes 4259856 | tf_op jit(solution)/shard_map/all_gather | solution.py:137
  120.1 0.8 slice.205
  121.2 2.6 %fusion = f32[512,256]{1,0:T(8,128)S(1)} fusion(f32[8,520,256]{2,1,0:T(8,128)} %bitcast.76, f32[8,512]{1,0:T(8,128)S(1)} %mul.248), kind=kLoop, calls=%fused_computation.2 | loop fusion | flops 1966080 | bytes 4734976 | tf_op jit(solution)/shard_map/reduce_sum | solution.py:146
  123.9 0.3 fusion.16
  124.1 0.3 fusion.19
  124.4 0.2 fusion.9
  124.6 0.1 copy.70
  124.8 0.3 fusion.7
  125.2 0.2 multiply_reduce_fusion.1
  125.4 4.9 %convolution_convert_fusion = bf16[64,8192]{1,0:T(8,128)(2,1)S(1)} fusion(bf16[512,8192]{1,0:T(8,128)(2,1)} %param.29, f32[512]{0:T(512)S(1)} %copy-done.2, f32[64,512]{1,0:T(8,128)S(1)} %copy.72, bf16[64,512]{1,0:T(8,128)(2,1)S(1)} %copy-done), kind=kOutput, calls=%fused_computation | convolution fusion | flops 537657344 | bytes 9635840 | tf_op jit(solution)/shard_map/dot_general | solution.py:163
  130.7 38.7 %all_to_all.5 = bf16[16,65,512]{2,1,0:T(8,128)(2,1)S(1)} all-to-all(bf16[16,65,512]{2,1,0:T(8,128)(2,1)S(1)} %pad_maximum_fusion), channel_id=1, replica_groups=mesh['cy'=8,'cz'=8,'tp'=16] {'tp'}, dimensions={0} | all-to-all | bytes 2129920 | tf_op jit(solution)/shard_map/all_to_all | solution.py:172
  169.6 0.9 multiply_reduce_fusion
  (69 shorter events, 2.7 us)
Async XLA Ops:
  6.5 17.2 %copy-start.1 = (bf16[64,512]{1,0:T(8,128)(2,1)S(1)}, bf16[64,512]{1,0:T(8,128)(2,1)}, u32[]{:S(2)}) copy-start(bf16[64,512]{1,0:T(8,128)(2,1)} %param.18) | copy-start | bytes 196612
  6.5 113.6 %all-gather.5.cloned.1.call-start = ((), (), s32[]{:S(2)}) async-start(), calls=%async_computation.1 | async-start | bytes 4792320 | tf_op jit(solution)/shard_map/all_gather | solution.py:137
  7.7 15.9 %collective-permute-start.1 = (bf16[3,512]{1,0:T(4,128)(2,1)S(1)}, bf16[3,512]{1,0:T(4,128)(2,1)S(1)}, u32[]{:S(2)}, u32[]{:S(2)}) collective-permute-start(bf16[3,512]{1,0:T(4,128)(2,1)S(1)} %pad_maximum_fusion.1), channel_id=1, source_target_pairs={{0,16},{16,32},{32,48},{48,64},{64,80},{80,96},{96,112},{112,128},... | collective-permute-start | bytes 9224 | tf_op jit(solution)/shard_map/ppermute | solution.py:17
  14.2 9.6 %collective-permute-start = (bf16[3,512]{1,0:T(4,128)(2,1)S(1)}, bf16[3,512]{1,0:T(4,128)(2,1)S(1)}, u32[]{:S(2)}, u32[]{:S(2)}) collective-permute-start(bf16[3,512]{1,0:T(4,128)(2,1)S(1)} %slice.145), channel_id=1, source_target_pairs={{0,16},{16,32},{32,48},{48,64},{64,80},{80,96},{96,112},{112,128},... | collective-permute-start | bytes 9224 | tf_op jit(solution)/shard_map/ppermute | solution.py:17
  123.8 0.9 copy-start.3
  123.9 1.3 copy-start
  123.9 1.5 copy-start.2
Sparse Core Ops, SparseCore 0:
  54.5 65.6 all-gather.4
